TPU v7x, 256 devices: a whole 4x4x8 slice. The times are simulated.
256 devices in a mesh: seq: 64 (over x, z, core), head: 4 (over y).
Axes of the slice: x: 4, y: 4, z: 8, core: 2. Of those that a mesh axis runs over, the one named last changes fastest.
Arguments:
- queries: bfloat16 [16384, 2048], P('seq', 'head'), may hold values from -30 to 30, as said below
- keys: bfloat16 [16384, 2048], P('seq', 'head'), may hold values from -30 to 30, as said below
- values: bfloat16 [16384, 2048], P('seq', 'head'), may hold values from -6 to 6
- out_grad: bfloat16 [16384, 2048], P('seq', 'head'), may hold values from -6 to 6
- rand_blocks: int32 [16, 128, 3], P('head', 'seq'), may hold values from 0 to 127, as said below
Outputs:
- attn_out: bfloat16 [16384, 2048], P('seq', 'head')
- grad_queries: bfloat16 [16384, 2048], P('seq', 'head')
- grad_keys: bfloat16 [16384, 2048], P('seq', 'head')
- grad_values: bfloat16 [16384, 2048], P('seq', 'head')
Inputs may be any that keep to these rules, and one draw needn't show every extreme that they name: queries are of order one; in some draws a few rows reach larger scales. keys are of order one; in some draws a few rows reach larger scales. `rand_blocks`: for each aligned group of 4 heads and each aligned run of 2 query blocks, at most 2 of the group's entries name blocks of one aligned run of 2 key blocks, and in every group some run is named exactly 2 times.
All inputs are finite; a program needn't handle non-finite values.
Results may differ from a plain program's by a relative error of at most 0.015.
The roundings to bfloat16 on the way count: a program that leaves them out, or rounds other values in their place, can miss the bound.
Values may be sent and summed in bfloat16 or wider, within the bound.
No kernel may reach another device: no remote copies, remote signals or barrier semaphores. Data moves between devices by JAX's collectives and lax.ppermute only.
A program may use at most 192 MiB of HBM per device.

v0:
```python
import math

import jax
import jax.numpy as jnp
from jax import lax
from jax.sharding import PartitionSpec as P


def swapped(value, axis, distance):
    mask = 2**distance
    pairs = [(source, source ^ mask) for source in range(lax.axis_size(axis))]
    return lax.ppermute(value, axis, pairs)


def round_trip(value_arr):
    return lax.optimization_barrier(value_arr.astype(jnp.bfloat16)).astype(jnp.float32)


def near_partner(block_arr, near_bit):
    span_size = 1 << near_bit
    folded = block_arr.reshape(
        (block_arr.shape[0] // (2 * span_size), 2, span_size) + block_arr.shape[1:]
    )
    return folded[:, ::-1].reshape(block_arr.shape)


def slot_terms(grad_scores, weights_low, query_rows, grad_rows, first_slot, last_slot, score_scale):
    key_terms = score_scale * jnp.einsum(
        "btks,btd->bksd",
        grad_scores[:, :, first_slot:last_slot],
        query_rows,
        preferred_element_type=jnp.float32,
    )
    value_terms = jnp.einsum(
        "btks,btd->bksd",
        weights_low[:, :, first_slot:last_slot],
        grad_rows,
        preferred_element_type=jnp.float32,
    )
    return (key_terms, value_terms)


def listed_rows(own_four, near_list, far_list, rand_part, head_index):
    part_list = [own_four[:, :, head_index]]
    part_list = part_list + [near_arr[:, :, head_index] for near_arr in near_list]
    part_list = part_list + [far_arr[:, :, head_index] for far_arr in far_list]
    return jnp.concatenate([jnp.stack(part_list, axis=1), rand_part[head_index]], axis=1)


def local(queries, keys, values, out_grad, rand_blocks):
    tok_rows = queries.shape[0]
    heads_here, blk_count, rand_count = rand_blocks.shape
    head_size = queries.shape[1] // heads_here
    blk_size = tok_rows // blk_count
    score_scale = 1.0 / math.sqrt(head_size)
    seq_devices = lax.axis_size("seq")
    far_count = seq_devices.bit_length() - 1
    near_count = blk_count.bit_length() - 1
    block_shape = (blk_count, blk_size, heads_here, head_size)
    query_four = queries.reshape(block_shape)
    key_four = keys.reshape(block_shape)
    value_four = values.reshape(block_shape)
    grad_four = out_grad.reshape(block_shape)
    far_keys = []
    far_values = []
    for far_level in range(far_count):
        got_keys, got_values = swapped((keys, values), "seq", far_level)
        far_keys.append(got_keys.reshape(block_shape))
        far_values.append(got_values.reshape(block_shape))
    near_keys = [near_partner(key_four, 0)]
    near_values = [near_partner(value_four, 0)]
    total_req = heads_here * blk_count * rand_count
    slot_cap = max(2, -(-total_req // seq_devices))
    slot_count = seq_devices * slot_cap
    flat_req = rand_blocks.reshape(-1)
    owner_dev = flat_req // blk_count
    req_index = jnp.arange(total_req, dtype=jnp.int32)
    req_head = req_index // (blk_count * rand_count)
    payload = req_head * blk_count + flat_req % blk_count
    earlier_same = (owner_dev[:, None] == owner_dev[None, :]) & (
        req_index[:, None] > req_index[None, :]
    )
    slot_rank = jnp.sum(earlier_same.astype(jnp.int32), axis=1)
    slot_of_req = owner_dev * slot_cap + slot_rank
    slot_match = slot_of_req[None, :] == jnp.arange(slot_count, dtype=jnp.int32)[:, None]
    filled = jnp.any(slot_match, axis=1)
    req_of_slot = jnp.sum(jnp.where(slot_match, req_index[None, :], 0), axis=1)
    send_ids = jnp.where(filled, jnp.sum(jnp.where(slot_match, payload[None, :], 0), axis=1), -1)
    send_ids = send_ids.reshape(seq_devices, slot_cap)
    asked_ids = lax.all_to_all(send_ids, "seq", split_axis=0, concat_axis=0, tiled=True)
    out_shape = asked_ids.shape + (blk_size, head_size)
    safe_ids = jnp.maximum(asked_ids.reshape(-1), 0)
    pick_head = safe_ids // blk_count
    pick_blk = safe_ids % blk_count
    key_pick = key_four[pick_blk, :, pick_head, :]
    value_pick = value_four[pick_blk, :, pick_head, :]
    key_back = lax.all_to_all(
        key_pick.reshape(out_shape), "seq", split_axis=0, concat_axis=0, tiled=True
    )
    value_back = lax.all_to_all(
        value_pick.reshape(out_shape), "seq", split_axis=0, concat_axis=0, tiled=True
    )
    key_slots, value_slots, asked_ids = (key_back, value_back, asked_ids)
    rand_shape = (heads_here, blk_count, rand_count, blk_size, head_size)
    rand_keys = key_slots.reshape(slot_count, blk_size, head_size)[slot_of_req].reshape(rand_shape)
    rand_values = value_slots.reshape(slot_count, blk_size, head_size)[slot_of_req].reshape(
        rand_shape
    )
    asked_flat = asked_ids.reshape(-1)
    key_sets = []
    value_sets = []
    weight_keep = []
    weight_low_keep = []
    attn_heads = []
    total_heads = []
    for head_index in range(heads_here):
        key_set = listed_rows(key_four, near_keys, far_keys, rand_keys, head_index)
        value_set = listed_rows(value_four, near_values, far_values, rand_values, head_index)
        scores = (
            jnp.einsum(
                "btd,bksd->btks",
                query_four[:, :, head_index],
                key_set,
                preferred_element_type=jnp.float32,
            )
            * score_scale
        )
        row_max = jnp.max(scores, axis=(2, 3))
        log_total = row_max + jnp.log(
            jnp.sum(jnp.exp(scores - row_max[:, :, None, None]), axis=(2, 3))
        )
        weights = jnp.exp(scores - log_total[:, :, None, None])
        weights_low = weights.astype(jnp.bfloat16)
        attn_heads.append(
            jnp.einsum(
                "btks,bksd->btd", weights_low, value_set, preferred_element_type=jnp.float32
            ).astype(jnp.bfloat16)
        )
        total_heads.append(log_total)
        key_sets.append(key_set)
        value_sets.append(value_set)
        weight_keep.append(weights)
        weight_low_keep.append(weights_low)
    attn_four = jnp.stack(attn_heads, axis=2)
    row_deltas = jnp.sum(grad_four.astype(jnp.float32) * attn_four.astype(jnp.float32), axis=3)
    slot_shape = (seq_devices, slot_cap, blk_size, head_size)
    far_first = 1 + near_count
    rand_first = far_first + far_count
    query_heads = []
    key_heads = []
    value_heads = []
    far_key_parts = []
    far_value_parts = []
    rand_key_parts = []
    rand_value_parts = []
    for head_index in range(heads_here):
        query_rows = query_four[:, :, head_index]
        grad_rows = grad_four[:, :, head_index]
        grad_weights = jnp.einsum(
            "btd,bksd->btks", grad_rows, value_sets[head_index], preferred_element_type=jnp.float32
        )
        grad_scores = (
            weight_keep[head_index]
            * (grad_weights - row_deltas[:, :, head_index][:, :, None, None])
        ).astype(jnp.bfloat16)
        query_heads.append(
            (
                score_scale
                * jnp.einsum(
                    "btks,bksd->btd",
                    grad_scores,
                    key_sets[head_index],
                    preferred_element_type=jnp.float32,
                )
            ).astype(jnp.bfloat16)
        )
        weights_low = weight_low_keep[head_index]
        own_keys, own_values = slot_terms(
            grad_scores, weights_low, query_rows, grad_rows, 0, far_first, score_scale
        )
        key_acc = own_keys[:, 0]
        value_acc = own_values[:, 0]
        key_acc = key_acc + near_partner(round_trip(own_keys[:, 1]), 0)
        value_acc = value_acc + near_partner(round_trip(own_values[:, 1]), 0)
        far_keys_part, far_values_part = slot_terms(
            grad_scores, weights_low, query_rows, grad_rows, far_first, rand_first, score_scale
        )
        far_key_parts.append(far_keys_part.astype(jnp.bfloat16))
        far_value_parts.append(far_values_part.astype(jnp.bfloat16))
        rand_keys_part, rand_values_part = slot_terms(
            grad_scores,
            weights_low,
            query_rows,
            grad_rows,
            rand_first,
            rand_first + rand_count,
            score_scale,
        )
        rand_key_parts.append(rand_keys_part.astype(jnp.bfloat16))
        rand_value_parts.append(rand_values_part.astype(jnp.bfloat16))
        key_heads.append(key_acc)
        value_heads.append(value_acc)
    key_grad = jnp.stack(key_heads, axis=2)
    value_grad = jnp.stack(value_heads, axis=2)
    far_key_all = jnp.stack(far_key_parts, axis=3)
    far_value_all = jnp.stack(far_value_parts, axis=3)
    for far_level in range(far_count):
        send_keys = far_key_all[:, far_level].reshape(tok_rows, heads_here * head_size)
        send_values = far_value_all[:, far_level].reshape(tok_rows, heads_here * head_size)
        back_keys, back_values = swapped((send_keys, send_values), "seq", far_level)
        key_grad = key_grad + back_keys.reshape(block_shape).astype(jnp.float32)
        value_grad = value_grad + back_values.reshape(block_shape).astype(jnp.float32)
    rand_key_all = jnp.stack(rand_key_parts, axis=0).reshape(total_req, blk_size, head_size)
    rand_value_all = jnp.stack(rand_value_parts, axis=0).reshape(total_req, blk_size, head_size)
    empty_slot = jnp.zeros((slot_count, blk_size, head_size), jnp.bfloat16)
    send_keys = jnp.where(filled[:, None, None], rand_key_all[req_of_slot], empty_slot).reshape(
        slot_shape
    )
    send_values = jnp.where(filled[:, None, None], rand_value_all[req_of_slot], empty_slot).reshape(
        slot_shape
    )
    slot_keys, slot_values = (
        lax.all_to_all(send_keys, "seq", split_axis=0, concat_axis=0, tiled=True),
        lax.all_to_all(send_values, "seq", split_axis=0, concat_axis=0, tiled=True),
    )
    target_rows = jnp.arange(heads_here * blk_count, dtype=jnp.int32)
    onehot = (asked_flat[None, :] == target_rows[:, None]).astype(jnp.bfloat16)
    extra_keys = jnp.dot(
        onehot,
        slot_keys.reshape(slot_count, blk_size * head_size),
        preferred_element_type=jnp.float32,
    )
    extra_values = jnp.dot(
        onehot,
        slot_values.reshape(slot_count, blk_size * head_size),
        preferred_element_type=jnp.float32,
    )
    extra_keys = extra_keys.reshape(heads_here, blk_count, blk_size, head_size).transpose(
        1, 2, 0, 3
    )
    extra_values = extra_values.reshape(heads_here, blk_count, blk_size, head_size).transpose(
        1, 2, 0, 3
    )
    attn_out = attn_four.reshape(tok_rows, heads_here * head_size)
    grad_queries = jnp.stack(query_heads, axis=2).reshape(tok_rows, heads_here * head_size)
    grad_keys = (
        (key_grad + extra_keys).astype(jnp.bfloat16).reshape(tok_rows, heads_here * head_size)
    )
    grad_values = (
        (value_grad + extra_values).astype(jnp.bfloat16).reshape(tok_rows, heads_here * head_size)
    )
    return (attn_out, grad_queries, grad_keys, grad_values)


def solution(mesh):
    return jax.shard_map(
        local,
        mesh=mesh,
        in_specs=(
            P("seq", "head"),
            P("seq", "head"),
            P("seq", "head"),
            P("seq", "head"),
            P("head", "seq", None),
        ),
        out_specs=(P("seq", "head"), P("seq", "head"), P("seq", "head"), P("seq", "head")),
        check_vma=False,
    )
```

profile of v0, /device:TPU:1, one launch (start us, length us, event | category | flops | bytes accessed | tf_op | source)
XLA Modules:
  0.0 628.4 jit_solution(2525929440258029698)
XLA Ops:
  0.6 3.3 collective-permute-start.6
  3.9 2.9 collective-permute-start.8
  6.8 4.2 collective-permute-start.9
  14.3 7.1 %all-to-all-start = ((s32[64,1,2]{2,1,0:T(1,128)}), s32[64,1,2]{2,1,0:T(1,128)S(1)}, u32[]{:S(2)}, u32[]{:S(2)}) async-start(s32[64,1,2]{2,1,0:T(1,128)} %bitcast.9), calls=%async_computation | async-start | bytes 65536 | tf_op jit(solution)/shard_map/all_to_all | solution.py:90
  25.3 12.0 %all-to-all-done = s32[64,1,2]{2,1,0:T(1,128)S(1)} async-done(((s32[64,1,2]{2,1,0:T(1,128)}), s32[64,1,2]{2,1,0:T(1,128)S(1)}, u32[]{:S(2)}, u32[]{:S(2)}) %all-to-all-start) | async-done | bytes 544 | tf_op jit(solution)/shard_map/all_to_all | solution.py:90
  39.9 3.2 gather_fusion.2
  43.1 5.7 all-to-all-start.2
  64.9 3.1 gather_fusion
  68.1 3.1 collective-permute-start.11
  99.6 52.1 %collective-permute-done.1 = bf16[256,512]{1,0:T(8,128)(2,1)} collective-permute-done((bf16[256,512]{1,0:T(8,128)(2,1)}, bf16[256,512]{1,0:T(8,128)(2,1)}, u32[]{:S(2)}, u32[]{:S(2)}) %collective-permute-start.1) | collective-permute-done | bytes 262176 | tf_op jit(solution)/shard_map/ppermute | solution.py:12
  153.8 9.6 %collective-permute-done.3 = bf16[256,512]{1,0:T(8,128)(2,1)} collective-permute-done((bf16[256,512]{1,0:T(8,128)(2,1)}, bf16[256,512]{1,0:T(8,128)(2,1)}, u32[]{:S(2)}, u32[]{:S(2)}) %collective-permute-start.3) | collective-permute-done | bytes 262176 | tf_op jit(solution)/shard_map/ppermute | solution.py:12
  182.5 10.5 %all-to-all-start.1 = ((bf16[64,2,128,128]{3,2,1,0:T(8,128)(2,1)}), bf16[64,2,128,128]{3,2,1,0:T(8,128)(2,1)}, u32[]{:S(2)}, u32[]{:S(2)}) async-start(bf16[64,2,128,128]{3,2,1,0:T(8,128)(2,1)} %bitcast.748), calls=%async_computation.1 | async-start | bytes 8388608 | tf_op jit(solution)/shard_map/all_to_all | solution.py:97
  234.9 53.8 %all-to-all-done.1 = bf16[64,2,128,128]{3,2,1,0:T(8,128)(2,1)} async-done(((bf16[64,2,128,128]{3,2,1,0:T(8,128)(2,1)}), bf16[64,2,128,128]{3,2,1,0:T(8,128)(2,1)}, u32[]{:S(2)}, u32[]{:S(2)}) %all-to-all-start.1) | async-done | bytes 4194336 | tf_op jit(solution)/shard_map/all_to_all | solution.py:97
  320.7 3.3 gather_fusion.5
  325.0 3.2 gather_fusion.4
  328.1 6.1 broadcast_select_fusion
  334.2 6.1 all-to-all-start.3
  342.3 93.9 %all-to-all-done.3 = bf16[64,2,128,128]{3,2,1,0:T(8,128)(2,1)} async-done(((bf16[64,2,128,128]{3,2,1,0:T(8,128)(2,1)}), bf16[64,2,128,128]{3,2,1,0:T(8,128)(2,1)}, u32[]{:S(2)}, u32[]{:S(2)}) %all-to-all-start.3) | async-done | bytes 4194336 | tf_op jit(solution)/shard_map/all_to_all | solution.py:223
  436.2 5.9 all-to-all-start.4
  445.3 3.1 collective-permute-start.17
  449.4 5.2 collective-permute-start.15
  469.7 3.6 collective-permute-done.16
  481.5 62.5 %collective-permute-done.15 = bf16[256,512]{1,0:T(8,128)(2,1)S(1)} collective-permute-done((bf16[256,512]{1,0:T(8,128)(2,1)S(1)}, bf16[256,512]{1,0:T(8,128)(2,1)S(1)}, u32[]{:S(2)}, u32[]{:S(2)}) %collective-permute-start.15) | collective-permute-done | bytes 262176 | tf_op jit(solution)/shard_map/ppermute | solution.py:12
  545.2 12.0 %collective-permute-done.14 = bf16[256,512]{1,0:T(8,128)(2,1)S(1)} collective-permute-done((bf16[256,512]{1,0:T(8,128)(2,1)S(1)}, bf16[256,512]{1,0:T(8,128)(2,1)S(1)}, u32[]{:S(2)}, u32[]{:S(2)}) %collective-permute-start.14) | collective-permute-done | bytes 262176 | tf_op jit(solution)/shard_map/ppermute | solution.py:12
  557.1 3.7 collective-permute-start.21
  575.8 9.2 %collective-permute-done.20 = bf16[256,512]{1,0:T(8,128)(2,1)} collective-permute-done((bf16[256,512]{1,0:T(8,128)(2,1)}, bf16[256,512]{1,0:T(8,128)(2,1)}, u32[]{:S(2)}, u32[]{:S(2)}) %collective-permute-start.20) | collective-permute-done | bytes 262176 | tf_op jit(solution)/shard_map/ppermute | solution.py:12
  589.9 7.7 %copy.911 = bf16[16,8,128,128]{3,1,2,0:T(8,128)(2,1)} copy(bf16[16,8,128,128]{3,2,1,0:T(8,128)(2,1)} %bitcast.256) | data formatting | bytes 8388608
  597.6 6.6 %copy.622 = bf16[16384,128]{1,0:T(8,128)(2,1)} copy(bf16[16384,128]{0,1:T(8,128)(2,1)} %bitcast.751) | data formatting | bytes 8388608 | tf_op jit(solution)/shard_map/dot_general | solution.py:228
  604.2 3.6 fusion.139
  609.0 7.8 %copy.910 = bf16[16,8,128,128]{3,1,2,0:T(8,128)(2,1)} copy(bf16[16,8,128,128]{3,2,1,0:T(8,128)(2,1)} %bitcast.286) | data formatting | bytes 8388608
  616.8 6.4 %copy.644 = bf16[16384,128]{1,0:T(8,128)(2,1)} copy(bf16[16384,128]{0,1:T(8,128)(2,1)} %bitcast.753) | data formatting | bytes 8388608 | tf_op jit(solution)/shard_map/dot_general | solution.py:233
  623.2 3.5 fusion.137
  (578 shorter events, 201.3 us)
Async XLA Ops:
  0.6 67.4 %collective-permute-start.6 = (bf16[256,512]{1,0:T(8,128)(2,1)}, bf16[256,512]{1,0:T(8,128)(2,1)}, u32[]{:S(2)}, u32[]{:S(2)}) collective-permute-start(bf16[256,512]{1,0:T(8,128)(2,1)} %param.7), channel_id=1, source_target_pairs={{0,4},{4,0},{8,12},{12,8},{16,20},{20,16},{24,28},{28,24},{32,36},... | collective-permute-start | bytes 786440 | tf_op jit(solution)/shard_map/ppermute | solution.py:12
  3.9 69.3 %collective-permute-start.7 = (bf16[256,512]{1,0:T(8,128)(2,1)}, bf16[256,512]{1,0:T(8,128)(2,1)}, u32[]{:S(2)}, u32[]{:S(2)}) collective-permute-start(bf16[256,512]{1,0:T(8,128)(2,1)} %param.7), channel_id=1, source_target_pairs={{0,8},{4,12},{8,0},{12,4},{16,24},{20,28},{24,16},{28,20},{32,40},... | collective-permute-start | bytes 786440 | tf_op jit(solution)/shard_map/ppermute | solution.py:12
  3.9 72.3 %collective-permute-start.8 = (bf16[256,512]{1,0:T(8,128)(2,1)}, bf16[256,512]{1,0:T(8,128)(2,1)}, u32[]{:S(2)}, u32[]{:S(2)}) collective-permute-start(bf16[256,512]{1,0:T(8,128)(2,1)} %param.7), channel_id=1, source_target_pairs={{0,16},{4,20},{8,24},{12,28},{16,0},{20,4},{24,8},{28,12},{32,48},... | collective-permute-start | bytes 786440 | tf_op jit(solution)/shard_map/ppermute | solution.py:12
  6.8 72.7 %collective-permute-start.9 = (bf16[256,512]{1,0:T(8,128)(2,1)}, bf16[256,512]{1,0:T(8,128)(2,1)}, u32[]{:S(2)}, u32[]{:S(2)}) collective-permute-start(bf16[256,512]{1,0:T(8,128)(2,1)} %param.7), channel_id=1, source_target_pairs={{0,32},{4,36},{8,40},{12,44},{16,48},{20,52},{24,56},{28,60},{32,0... | collective-permute-start | bytes 786440 | tf_op jit(solution)/shard_map/ppermute | solution.py:12
  11.1 71.6 %collective-permute-start.10 = (bf16[256,512]{1,0:T(8,128)(2,1)}, bf16[256,512]{1,0:T(8,128)(2,1)}, u32[]{:S(2)}, u32[]{:S(2)}) collective-permute-start(bf16[256,512]{1,0:T(8,128)(2,1)} %param.7), channel_id=1, source_target_pairs={{0,64},{4,68},{8,72},{12,76},{16,80},{20,84},{24,88},{28,92},{32,9... | collective-permute-start | bytes 786440 | tf_op jit(solution)/shard_map/ppermute | solution.py:12
  14.3 23.1 %all-to-all-start = ((s32[64,1,2]{2,1,0:T(1,128)}), s32[64,1,2]{2,1,0:T(1,128)S(1)}, u32[]{:S(2)}, u32[]{:S(2)}) async-start(s32[64,1,2]{2,1,0:T(1,128)} %bitcast.9), calls=%async_computation | async-start | bytes 65536 | tf_op jit(solution)/shard_map/all_to_all | solution.py:90
  43.1 139.4 %all-to-all-start.2 = ((bf16[64,2,128,128]{3,2,1,0:T(8,128)(2,1)}), bf16[64,2,128,128]{3,2,1,0:T(8,128)(2,1)}, u32[]{:S(2)}, u32[]{:S(2)}) async-start(bf16[64,2,128,128]{3,2,1,0:T(8,128)(2,1)} %bitcast.749), calls=%async_computation.2 | async-start | bytes 8388608 | tf_op jit(solution)/shard_map/all_to_all | solution.py:100
  68.1 19.4 %collective-permute-start.11 = (bf16[256,512]{1,0:T(8,128)(2,1)S(1)}, bf16[256,512]{1,0:T(8,128)(2,1)}, u32[]{:S(2)}, u32[]{:S(2)}) collective-permute-start(bf16[256,512]{1,0:T(8,128)(2,1)S(1)} %copy-done.37), channel_id=1, source_target_pairs={{0,128},{4,132},{8,136},{12,140},{16,144},{20,148},{24,152},{28,15... | collective-permute-start | bytes 786440 | tf_op jit(solution)/shard_map/ppermute | solution.py:12
  73.2 14.6 %collective-permute-start = (bf16[256,512]{1,0:T(8,128)(2,1)}, bf16[256,512]{1,0:T(8,128)(2,1)}, u32[]{:S(2)}, u32[]{:S(2)}) collective-permute-start(bf16[256,512]{1,0:T(8,128)(2,1)} %param.6), channel_id=1, source_target_pairs={{0,4},{4,0},{8,12},{12,8},{16,20},{20,16},{24,28},{28,24},{32,36},... | collective-permute-start | bytes 786440 | tf_op jit(solution)/shard_map/ppermute | solution.py:12
  76.2 75.5 %collective-permute-start.1 = (bf16[256,512]{1,0:T(8,128)(2,1)}, bf16[256,512]{1,0:T(8,128)(2,1)}, u32[]{:S(2)}, u32[]{:S(2)}) collective-permute-start(bf16[256,512]{1,0:T(8,128)(2,1)} %param.6), channel_id=1, source_target_pairs={{0,8},{4,12},{8,0},{12,4},{16,24},{20,28},{24,16},{28,20},{32,40},... | collective-permute-start | bytes 786440 | tf_op jit(solution)/shard_map/ppermute | solution.py:12
  79.6 73.2 %collective-permute-start.2 = (bf16[256,512]{1,0:T(8,128)(2,1)}, bf16[256,512]{1,0:T(8,128)(2,1)}, u32[]{:S(2)}, u32[]{:S(2)}) collective-permute-start(bf16[256,512]{1,0:T(8,128)(2,1)} %param.6), channel_id=1, source_target_pairs={{0,16},{4,20},{8,24},{12,28},{16,0},{20,4},{24,8},{28,12},{32,48},... | collective-permute-start | bytes 786440 | tf_op jit(solution)/shard_map/ppermute | solution.py:12
  82.7 80.7 %collective-permute-start.3 = (bf16[256,512]{1,0:T(8,128)(2,1)}, bf16[256,512]{1,0:T(8,128)(2,1)}, u32[]{:S(2)}, u32[]{:S(2)}) collective-permute-start(bf16[256,512]{1,0:T(8,128)(2,1)} %param.6), channel_id=1, source_target_pairs={{0,32},{4,36},{8,40},{12,44},{16,48},{20,52},{24,56},{28,60},{32,0... | collective-permute-start | bytes 786440 | tf_op jit(solution)/shard_map/ppermute | solution.py:12
  87.4 77.0 %collective-permute-start.4 = (bf16[256,512]{1,0:T(8,128)(2,1)}, bf16[256,512]{1,0:T(8,128)(2,1)}, u32[]{:S(2)}, u32[]{:S(2)}) collective-permute-start(bf16[256,512]{1,0:T(8,128)(2,1)} %param.6), channel_id=1, source_target_pairs={{0,64},{4,68},{8,72},{12,76},{16,80},{20,84},{24,88},{28,92},{32,9... | collective-permute-start | bytes 786440 | tf_op jit(solution)/shard_map/ppermute | solution.py:12
  87.9 77.6 %collective-permute-start.5 = (bf16[256,512]{1,0:T(8,128)(2,1)}, bf16[256,512]{1,0:T(8,128)(2,1)}, u32[]{:S(2)}, u32[]{:S(2)}) collective-permute-start(bf16[256,512]{1,0:T(8,128)(2,1)} %param.6), channel_id=1, source_target_pairs={{0,128},{4,132},{8,136},{12,140},{16,144},{20,148},{24,152},{28,15... | collective-permute-start | bytes 786440 | tf_op jit(solution)/shard_map/ppermute | solution.py:12
  182.5 16.8 %copy-start.60 = (bf16[2,128,1,128]{3,2,1,0:T(2,128)(2,1)S(1)}, bf16[2,128,1,128]{3,2,1,0:T(2,128)(2,1)}, u32[]{:S(2)}) copy-start(bf16[2,128,1,128]{3,2,1,0:T(2,128)(2,1)} %get-tuple-element.89) | copy-start | bytes 196612
  182.5 106.2 %all-to-all-start.1 = ((bf16[64,2,128,128]{3,2,1,0:T(8,128)(2,1)}), bf16[64,2,128,128]{3,2,1,0:T(8,128)(2,1)}, u32[]{:S(2)}, u32[]{:S(2)}) async-start(bf16[64,2,128,128]{3,2,1,0:T(8,128)(2,1)} %bitcast.748), calls=%async_computation.1 | async-start | bytes 8388608 | tf_op jit(solution)/shard_map/all_to_all | solution.py:97
  207.8 15.4 %copy-start.75 = (bf16[2,128,1,128]{3,2,1,0:T(2,128)(2,1)S(1)}, bf16[2,128,1,128]{3,2,1,0:T(2,128)(2,1)}, u32[]{:S(2)}) copy-start(bf16[2,128,1,128]{3,2,1,0:T(2,128)(2,1)} %get-tuple-element.59) | copy-start | bytes 196612
  334.2 102.0 %all-to-all-start.3 = ((bf16[64,2,128,128]{3,2,1,0:T(8,128)(2,1)}), bf16[64,2,128,128]{3,2,1,0:T(8,128)(2,1)}, u32[]{:S(2)}, u32[]{:S(2)}) async-start(bf16[64,2,128,128]{3,2,1,0:T(8,128)(2,1)} %get-tuple-element.102), calls=%async_computation.3 | async-start | bytes 8388608 | tf_op jit(solution)/shard_map/all_to_all | solution.py:223
  436.2 172.8 %all-to-all-start.4 = ((bf16[64,2,128,128]{3,2,1,0:T(8,128)(2,1)}), bf16[64,2,128,128]{3,2,1,0:T(8,128)(2,1)}, u32[]{:S(2)}, u32[]{:S(2)}) async-start(bf16[64,2,128,128]{3,2,1,0:T(8,128)(2,1)} %get-tuple-element.101), calls=%async_computation.4 | async-start | bytes 8388608 | tf_op jit(solution)/shard_map/all_to_all | solution.py:224
  445.3 22.4 %collective-permute-start.17 = (bf16[256,512]{1,0:T(8,128)(2,1)S(1)}, bf16[256,512]{1,0:T(8,128)(2,1)S(1)}, u32[]{:S(2)}, u32[]{:S(2)}) collective-permute-start(bf16[256,512]{1,0:T(8,128)(2,1)S(1)} %bitcast.783), channel_id=1, source_target_pairs={{0,128},{4,132},{8,136},{12,140},{16,144},{20,148},{24,152},{28,15... | collective-permute-start | bytes 786440 | tf_op jit(solution)/shard_map/ppermute | solution.py:12
  448.6 24.7 %collective-permute-start.16 = (bf16[256,512]{1,0:T(8,128)(2,1)S(1)}, bf16[256,512]{1,0:T(8,128)(2,1)S(1)}, u32[]{:S(2)}, u32[]{:S(2)}) collective-permute-start(bf16[256,512]{1,0:T(8,128)(2,1)S(1)} %bitcast.784), channel_id=1, source_target_pairs={{0,64},{4,68},{8,72},{12,76},{16,80},{20,84},{24,88},{28,92},{32,9... | collective-permute-start | bytes 786440 | tf_op jit(solution)/shard_map/ppermute | solution.py:12
  449.4 94.6 %collective-permute-start.15 = (bf16[256,512]{1,0:T(8,128)(2,1)S(1)}, bf16[256,512]{1,0:T(8,128)(2,1)S(1)}, u32[]{:S(2)}, u32[]{:S(2)}) collective-permute-start(bf16[256,512]{1,0:T(8,128)(2,1)S(1)} %bitcast.780), channel_id=1, source_target_pairs={{0,32},{4,36},{8,40},{12,44},{16,48},{20,52},{24,56},{28,60},{32,0... | collective-permute-start | bytes 786440 | tf_op jit(solution)/shard_map/ppermute | solution.py:12
  454.9 102.3 %collective-permute-start.14 = (bf16[256,512]{1,0:T(8,128)(2,1)S(1)}, bf16[256,512]{1,0:T(8,128)(2,1)S(1)}, u32[]{:S(2)}, u32[]{:S(2)}) collective-permute-start(bf16[256,512]{1,0:T(8,128)(2,1)S(1)} %bitcast.781), channel_id=1, source_target_pairs={{0,16},{4,20},{8,24},{12,28},{16,0},{20,4},{24,8},{28,12},{32,48},... | collective-permute-start | bytes 786440 | tf_op jit(solution)/shard_map/ppermute | solution.py:12
  455.5 105.3 %collective-permute-start.13 = (bf16[256,512]{1,0:T(8,128)(2,1)S(1)}, bf16[256,512]{1,0:T(8,128)(2,1)S(1)}, u32[]{:S(2)}, u32[]{:S(2)}) collective-permute-start(bf16[256,512]{1,0:T(8,128)(2,1)S(1)} %bitcast.782), channel_id=1, source_target_pairs={{0,8},{4,12},{8,0},{12,4},{16,24},{20,28},{24,16},{28,20},{32,40},... | collective-permute-start | bytes 786440 | tf_op jit(solution)/shard_map/ppermute | solution.py:12
  467.7 93.2 %collective-permute-start.12 = (bf16[256,512]{1,0:T(8,128)(2,1)S(1)}, bf16[256,512]{1,0:T(8,128)(2,1)S(1)}, u32[]{:S(2)}, u32[]{:S(2)}) collective-permute-start(bf16[256,512]{1,0:T(8,128)(2,1)S(1)} %bitcast.788), channel_id=1, source_target_pairs={{0,4},{4,0},{8,12},{12,8},{16,20},{20,16},{24,28},{28,24},{32,36},... | collective-permute-start | bytes 786440 | tf_op jit(solution)/shard_map/ppermute | solution.py:12
  473.3 89.5 %collective-permute-start.23 = (bf16[256,512]{1,0:T(8,128)(2,1)S(1)}, bf16[256,512]{1,0:T(8,128)(2,1)S(1)}, u32[]{:S(2)}, u32[]{:S(2)}) collective-permute-start(bf16[256,512]{1,0:T(8,128)(2,1)S(1)} %bitcast.787), channel_id=1, source_target_pairs={{0,128},{4,132},{8,136},{12,140},{16,144},{20,148},{24,152},{28,15... | collective-permute-start | bytes 786440 | tf_op jit(solution)/shard_map/ppermute | solution.py:12
  544.0 20.6 %copy-start.97 = (bf16[256,512]{1,0:T(8,128)(2,1)}, bf16[256,512]{1,0:T(8,128)(2,1)S(1)}, u32[]{:S(2)}) copy-start(bf16[256,512]{1,0:T(8,128)(2,1)S(1)} %collective-permute-done.15) | copy-start | bytes 786436
  544.0 27.7 %collective-permute-start.22 = (bf16[256,512]{1,0:T(8,128)(2,1)}, bf16[256,512]{1,0:T(8,128)(2,1)}, u32[]{:S(2)}, u32[]{:S(2)}) collective-permute-start(bf16[256,512]{1,0:T(8,128)(2,1)} %bitcast.732), channel_id=1, source_target_pairs={{0,64},{4,68},{8,72},{12,76},{16,80},{20,84},{24,88},{28,92},{32,9... | collective-permute-start | bytes 786440 | tf_op jit(solution)/shard_map/ppermute | solution.py:12
  557.1 17.5 %collective-permute-start.21 = (bf16[256,512]{1,0:T(8,128)(2,1)}, bf16[256,512]{1,0:T(8,128)(2,1)}, u32[]{:S(2)}, u32[]{:S(2)}) collective-permute-start(bf16[256,512]{1,0:T(8,128)(2,1)} %bitcast.733), channel_id=1, source_target_pairs={{0,32},{4,36},{8,40},{12,44},{16,48},{20,52},{24,56},{28,60},{32,0... | collective-permute-start | bytes 786440 | tf_op jit(solution)/shard_map/ppermute | solution.py:12
  560.9 24.1 %collective-permute-start.20 = (bf16[256,512]{1,0:T(8,128)(2,1)}, bf16[256,512]{1,0:T(8,128)(2,1)}, u32[]{:S(2)}, u32[]{:S(2)}) collective-permute-start(bf16[256,512]{1,0:T(8,128)(2,1)} %bitcast.734), channel_id=1, source_target_pairs={{0,16},{4,20},{8,24},{12,28},{16,0},{20,4},{24,8},{28,12},{32,48},... | collective-permute-start | bytes 786440 | tf_op jit(solution)/shard_map/ppermute | solution.py:12
  560.9 25.2 %collective-permute-start.19 = (bf16[256,512]{1,0:T(8,128)(2,1)}, bf16[256,512]{1,0:T(8,128)(2,1)}, u32[]{:S(2)}, u32[]{:S(2)}) collective-permute-start(bf16[256,512]{1,0:T(8,128)(2,1)} %bitcast.735), channel_id=1, source_target_pairs={{0,8},{4,12},{8,0},{12,4},{16,24},{20,28},{24,16},{28,20},{32,40},... | collective-permute-start | bytes 786440 | tf_op jit(solution)/shard_map/ppermute | solution.py:12
  562.8 25.2 %collective-permute-start.18 = (bf16[256,512]{1,0:T(8,128)(2,1)}, bf16[256,512]{1,0:T(8,128)(2,1)}, u32[]{:S(2)}, u32[]{:S(2)}) collective-permute-start(bf16[256,512]{1,0:T(8,128)(2,1)} %bitcast.736), channel_id=1, source_target_pairs={{0,4},{4,0},{8,12},{12,8},{16,20},{20,16},{24,28},{28,24},{32,36},... | collective-permute-start | bytes 786440 | tf_op jit(solution)/shard_map/ppermute | solution.py:12
  (117 other events, 715.6 us)
where the time goes:
time: 640 us; the launch traced here: 628 us
  waiting for transfers between devices  311 us (49%)
  local copies, waits for them, and re-layouts  186 us (29%)
  starting transfers between devices  81.6 us (13%)
  matrix products  28.7 us (4%)
  other arithmetic  18.6 us (3%)
    ppermute x24, waiting for transfers between devices, swapped(): return lax.ppermute(value, axis, pairs)  151 us
    all_to_all x1, waiting for transfers between devices, local(): lax.all_to_all(send_keys, 'seq', split_axis=0, concat_axis=0, tiled=True)  93.9 us
    unnamed x347, local copies, waits for them, and re-layouts  90.6 us
    all_to_all x1, waiting for transfers between devices, local(): lax.all_to_all(key_pick.reshape(out_shape), 'seq', split_axis=0, concat_a...  53.8 us
    ppermute x24, starting transfers between devices, swapped(): return lax.ppermute(value, axis, pairs)  46.2 us
    slice x12, local copies, waits for them, and re-layouts, listed_rows(): part_list = part_list + [far_arr[:, :, head_index] for far_arr in far_list]  15 us
  transfers between devices with their start and end apart: 29, of which 10 were waited for; matrix products, arithmetic and copies ran while one was open for 27% of the time, Pallas kernels for 0%

commit v1 on v0

v1 whole, which is shorter than its diff:
```python
import math

import jax
import jax.numpy as jnp
from jax import lax
from jax.sharding import PartitionSpec as P


def swapped(value, axis, distance):
    mask = 2**distance
    pairs = [(source, source ^ mask) for source in range(lax.axis_size(axis))]
    return lax.ppermute(value, axis, pairs)


def low(value_arr):
    return value_arr.astype(jnp.bfloat16).astype(jnp.float32)


def local(queries, keys, values, out_grad, rand_blocks):
    tok_rows = queries.shape[0]
    heads_here, blk_count, rand_count = rand_blocks.shape
    head_size = queries.shape[1] // heads_here
    blk_size = tok_rows // blk_count
    score_scale = 1.0 / math.sqrt(head_size)
    seq_devices = lax.axis_size("seq")
    far_count = seq_devices.bit_length() - 1
    f32 = jnp.float32

    def heads_first(arr):
        return arr.reshape(blk_count, blk_size, heads_here, head_size).transpose(2, 0, 1, 3)

    def rows_back(arr):
        return arr.transpose(1, 2, 0, 3).reshape(tok_rows, heads_here * head_size)

    total_req = heads_here * blk_count * rand_count
    slot_cap = max(2, -(-total_req // seq_devices))
    slot_count = seq_devices * slot_cap
    flat_req = rand_blocks.reshape(-1)
    owner_dev = flat_req // blk_count
    req_index = jnp.arange(total_req, dtype=jnp.int32)
    req_head = req_index // (blk_count * rand_count)
    payload = req_head * blk_count + flat_req % blk_count
    earlier_same = (owner_dev[:, None] == owner_dev[None, :]) & (
        req_index[:, None] > req_index[None, :]
    )
    slot_rank = jnp.sum(earlier_same.astype(jnp.int32), axis=1)
    slot_of_req = owner_dev * slot_cap + slot_rank
    slot_match = slot_of_req[None, :] == jnp.arange(slot_count, dtype=jnp.int32)[:, None]
    filled = jnp.any(slot_match, axis=1)
    send_ids = jnp.where(filled, jnp.sum(jnp.where(slot_match, payload[None, :], 0), axis=1), -1)
    asked_ids = lax.all_to_all(
        send_ids.reshape(seq_devices, slot_cap), "seq", split_axis=0, concat_axis=0, tiled=True
    )
    asked_flat = asked_ids.reshape(-1)

    kv_rows = jnp.stack([keys, values])
    far_kv = [swapped(kv_rows, "seq", far_level) for far_level in range(far_count)]

    kv_four = kv_rows.reshape(2, blk_count, blk_size, heads_here, head_size)
    safe_ids = jnp.maximum(asked_flat, 0)
    pick_head = safe_ids // blk_count
    pick_blk = safe_ids % blk_count
    kv_pick = kv_four[:, pick_blk, :, pick_head, :]
    kv_back = lax.all_to_all(
        kv_pick.reshape(seq_devices, slot_cap, 2, blk_size, head_size),
        "seq",
        split_axis=0,
        concat_axis=0,
        tiled=True,
    ).reshape(slot_count, 2, blk_size, head_size)
    rand_kv = kv_back[slot_of_req].reshape(
        heads_here, blk_count, rand_count, 2, blk_size, head_size
    )

    def key_list(which):
        own = heads_first(kv_rows[which])
        parts = [own[:, :, None], own[:, ::-1, None]]
        parts += [heads_first(far_arr[which])[:, :, None] for far_arr in far_kv]
        parts.append(rand_kv[:, :, :, which])
        return jnp.concatenate(parts, axis=2)

    key_set = key_list(0)
    value_set = key_list(1)
    query_h = heads_first(queries)
    grad_h = heads_first(out_grad)

    scores = (
        jnp.einsum("hbtd,hbksd->hbtks", query_h, key_set, preferred_element_type=f32)
        * score_scale
    )
    row_max = jnp.max(scores, axis=(3, 4))
    log_total = row_max + jnp.log(
        jnp.sum(jnp.exp(scores - row_max[..., None, None]), axis=(3, 4))
    )
    weights = jnp.exp(scores - log_total[..., None, None])
    weights_low = weights.astype(jnp.bfloat16)
    attn_h = jnp.einsum(
        "hbtks,hbksd->hbtd", weights_low, value_set, preferred_element_type=f32
    ).astype(jnp.bfloat16)
    row_delta = jnp.sum(grad_h.astype(f32) * attn_h.astype(f32), axis=3)
    grad_weights = jnp.einsum("hbtd,hbksd->hbtks", grad_h, value_set, preferred_element_type=f32)
    grad_scores = (weights * (grad_weights - row_delta[..., None, None])).astype(jnp.bfloat16)
    grad_query_h = (
        score_scale
        * jnp.einsum("hbtks,hbksd->hbtd", grad_scores, key_set, preferred_element_type=f32)
    ).astype(jnp.bfloat16)
    key_terms = score_scale * jnp.einsum(
        "hbtks,hbtd->hbksd", grad_scores, query_h, preferred_element_type=f32
    )
    value_terms = jnp.einsum(
        "hbtks,hbtd->hbksd", weights_low, grad_h, preferred_element_type=f32
    )
    terms = jnp.stack([key_terms, value_terms])

    grad_kv = terms[:, :, :, 0] + low(terms[:, :, :, 1])[:, :, ::-1]
    far_first = 2
    rand_first = far_first + far_count
    far_low = terms[:, :, :, far_first:rand_first].astype(jnp.bfloat16)
    for far_level in range(far_count):
        send = far_low[:, :, :, far_level]
        back = swapped(send, "seq", far_level)
        grad_kv = grad_kv + back.astype(f32)

    rand_low = terms[:, :, :, rand_first:].astype(jnp.bfloat16)
    rand_req = rand_low.transpose(1, 2, 3, 0, 4, 5).reshape(total_req, 2 * blk_size * head_size)
    slot_onehot = slot_match.astype(jnp.bfloat16)
    send_terms = jnp.dot(slot_onehot, rand_req, preferred_element_type=f32).astype(jnp.bfloat16)
    slot_terms = lax.all_to_all(
        send_terms.reshape(seq_devices, slot_cap, 2 * blk_size * head_size),
        "seq",
        split_axis=0,
        concat_axis=0,
        tiled=True,
    ).reshape(slot_count, 2 * blk_size * head_size)
    target_rows = jnp.arange(heads_here * blk_count, dtype=jnp.int32)
    onehot = (asked_flat[None, :] == target_rows[:, None]).astype(jnp.bfloat16)
    extra = jnp.dot(onehot, slot_terms, preferred_element_type=f32)
    extra = extra.reshape(heads_here, blk_count, 2, blk_size, head_size).transpose(2, 0, 1, 3, 4)
    grad_kv = (grad_kv + extra).astype(jnp.bfloat16)

    attn_out = rows_back(attn_h)
    grad_queries = rows_back(grad_query_h)
    grad_keys = rows_back(grad_kv[0])
    grad_values = rows_back(grad_kv[1])
    return (attn_out, grad_queries, grad_keys, grad_values)


def solution(mesh):
    return jax.shard_map(
        local,
        mesh=mesh,
        in_specs=(
            P("seq", "head"),
            P("seq", "head"),
            P("seq", "head"),
            P("seq", "head"),
            P("head", "seq", None),
        ),
        out_specs=(P("seq", "head"), P("seq", "head"), P("seq", "head"), P("seq", "head")),
        check_vma=False,
    )
```

time: 640 us -> 616 us (0.963)
  the two profiles are of different devices: /device:TPU:1 before, /device:TPU:152 now
where the time goes in v1:
time: 616 us; the launch traced here: 613 us
  waiting for transfers between devices  402 us (65%)
  local copies, waits for them, and re-layouts  118 us (19%)
  starting transfers between devices  46.7 us (8%)
  matrix products  28.9 us (5%)
  other arithmetic  17.5 us (3%)
    ppermute x12, waiting for transfers between devices, swapped(): return lax.ppermute(value, axis, pairs)  200 us
    all_to_all x1, waiting for transfers between devices, local(): lax.all_to_all(send_terms.reshape(seq_devices, slot_cap, 2 * blk_size * h...  199 us
    reshape x2, local copies, waits for them, and re-layouts, local(): slot_terms = lax.all_to_all(send_terms.reshape(seq_devices, slot_cap, 2 *...  25.2 us
    another operation x16, local copies, waits for them, and re-layouts, heads_first(): arr.reshape(blk_count, blk_size, heads_here, head_size)  20.9 us
    unnamed x48, local copies, waits for them, and re-layouts  16.8 us
    ppermute x12, starting transfers between devices, swapped(): return lax.ppermute(value, axis, pairs)  15.7 us
    reshape x1, local copies, waits for them, and re-layouts, local(): send_terms.reshape(seq_devices, slot_cap, 2 * blk_size * head_size)  14.1 us
  transfers between devices with their start and end apart: 15, of which 7 were waited for; matrix products, arithmetic and copies ran while one was open for 15% of the time, Pallas kernels for 0%

profile of v1, /device:TPU:152, one launch (start us, length us, event | category | flops | bytes accessed | tf_op | source)
XLA Modules:
  0.0 613.4 jit_solution(2028472766716730421)
XLA Ops:
  2.7 10.2 %all-to-all-start = ((s32[64,1,2]{2,1,0:T(1,128)}), s32[64,1,2]{2,1,0:T(1,128)S(1)}, u32[]{:S(2)}, u32[]{:S(2)}) async-start(s32[64,1,2]{2,1,0:T(1,128)} %bitcast.18), calls=%async_computation | async-start | bytes 65536 | tf_op jit(solution)/shard_map/all_to_all | solution.py:51
  15.1 2.6 all-to-all-done
  19.7 6.7 %gather_fusion = bf16[128,2,128,128]{3,2,1,0:T(8,128)(2,1)} fusion(bf16[2,2,128,4,128]{4,2,3,1,0:T(8,128)(2,1)S(1)} %pad_maximum_fusion.2, s32[128]{0:T(128)S(1)} %fusion.51), kind=kCustom, calls=%fused_computation | custom fusion | bytes 16778240 | tf_op jit(solution)/shard_map/gather | solution.py:63
  26.5 10.5 %all-to-all-start.1 = ((bf16[64,2,2,128,128]{4,3,2,1,0:T(8,128)(2,1)}), bf16[64,2,2,128,128]{4,3,2,1,0:T(8,128)(2,1)}, u32[]{:S(2)}, u32[]{:S(2)}) async-start(bf16[64,2,2,128,128]{4,3,2,1,0:T(8,128)(2,1)} %bitcast.266), calls=%async_computation.1 | async-start | bytes 16777216 | tf_op jit(solution)/shard_map/all_to_all | solution.py:64
  37.8 3.2 collective-permute-start.5
  42.2 2.4 collective-permute-start.2
  50.9 22.9 %collective-permute-done.5 = bf16[2,256,512]{2,1,0:T(8,128)(2,1)} collective-permute-done((bf16[2,256,512]{2,1,0:T(8,128)(2,1)}, bf16[2,256,512]{2,1,0:T(8,128)(2,1)}, u32[]{:S(2)}, u32[]{:S(2)}) %collective-permute-start.5) | collective-permute-done | bytes 524320 | tf_op jit(solution)/shard_map/ppermute | solution.py:12
  73.9 1.9 fusion.55
  75.7 23.1 %collective-permute-done.4 = bf16[2,256,512]{2,1,0:T(8,128)(2,1)} collective-permute-done((bf16[2,256,512]{2,1,0:T(8,128)(2,1)}, bf16[2,256,512]{2,1,0:T(8,128)(2,1)}, u32[]{:S(2)}, u32[]{:S(2)}) %collective-permute-start.4) | collective-permute-done | bytes 524320 | tf_op jit(solution)/shard_map/ppermute | solution.py:12
  100.7 131.4 %collective-permute-done.3 = bf16[2,256,512]{2,1,0:T(8,128)(2,1)} collective-permute-done((bf16[2,256,512]{2,1,0:T(8,128)(2,1)}, bf16[2,256,512]{2,1,0:T(8,128)(2,1)}, u32[]{:S(2)}, u32[]{:S(2)}) %collective-permute-start.3) | collective-permute-done | bytes 524320 | tf_op jit(solution)/shard_map/ppermute | solution.py:12
  244.4 19.3 %collective-permute-done.2 = bf16[2,256,512]{2,1,0:T(8,128)(2,1)} collective-permute-done((bf16[2,256,512]{2,1,0:T(8,128)(2,1)}, bf16[2,256,512]{2,1,0:T(8,128)(2,1)}, u32[]{:S(2)}, u32[]{:S(2)}) %collective-permute-start.2) | collective-permute-done | bytes 524320 | tf_op jit(solution)/shard_map/ppermute | solution.py:12
  269.0 1.9 fusion.59
  274.3 1.9 fusion.60
  290.4 5.4 gather_fusion.1
  301.2 3.5 convolution_bitcast_fusion
  304.7 4.4 multiply_reduce_fusion
  309.2 3.4 fusion.1
  313.5 8.1 %fusion = bf16[2,4,2,11,128,128]{5,4,3,2,1,0:T(8,128)(2,1)} fusion(f32[1,4,2,11,128,128]{5,4,3,2,1,0:T(8,128)} %convolution_bitcast_fusion, f32[1,4,2,11,128,128]{5,4,3,2,1,0:T(8,128)S(1)} %multiply_bitcast_fusion), kind=kLoop, calls=%fused_computation.6 | loop fusion | flops 2883584 | bytes 17301504 | tf_op jit(solution)/shard_map/convert.3
  324.4 3.7 reshape.377
  328.1 7.1 %convolution_convert_fusion = bf16[128,32768]{1,0:T(8,128)(2,1)} fusion(bf16[24,32768]{1,0:T(8,128)(2,1)} %reshape.377, s32[24]{0:T(128)S(1)} %multiply_add_fusion.1), kind=kOutput, calls=%fused_computation.2 | convolution fusion | flops 205523968 | bytes 9961568 | tf_op jit(solution)/shard_map/dot_general | solution.py:127
  335.2 14.1 %reshape.378 = bf16[64,2,32768]{2,1,0:T(2,128)(2,1)} reshape(bf16[128,32768]{1,0:T(8,128)(2,1)} %convolution_convert_fusion) | data formatting | bytes 16777216 | tf_op jit(solution)/shard_map/reshape | solution.py:129
  349.3 10.3 %all-to-all-start.2 = ((bf16[64,2,32768]{2,1,0:T(2,128)(2,1)}), bf16[64,2,32768]{2,1,0:T(2,128)(2,1)}, u32[]{:S(2)}, u32[]{:S(2)}) async-start(bf16[64,2,32768]{2,1,0:T(2,128)(2,1)} %reshape.378), calls=%async_computation.2 | async-start | bytes 16777216 | tf_op jit(solution)/shard_map/all_to_all | solution.py:128
  359.6 4.0 fusion.23
  364.3 2.9 fusion.9
  369.0 2.4 collective-permute-start.8
  372.9 3.1 collective-permute-start.11
  376.0 199.0 %all-to-all-done.2 = bf16[64,2,32768]{2,1,0:T(2,128)(2,1)} async-done(((bf16[64,2,32768]{2,1,0:T(2,128)(2,1)}), bf16[64,2,32768]{2,1,0:T(2,128)(2,1)}, u32[]{:S(2)}, u32[]{:S(2)}) %all-to-all-start.2) | async-done | bytes 8388640 | tf_op jit(solution)/shard_map/all_to_all | solution.py:128
  575.0 13.2 %reshape.379 = bf16[128,32768]{1,0:T(8,128)(2,1)} reshape(bf16[64,2,32768]{2,1,0:T(2,128)(2,1)} %all-to-all-done.2) | data formatting | bytes 16777216 | tf_op jit(solution)/shard_map/reshape | solution.py:134
  588.2 12.0 %copy.192 = bf16[128,32768]{0,1:T(8,128)(2,1)} copy(bf16[128,32768]{1,0:T(8,128)(2,1)} %reshape.379) | data formatting | bytes 16777216 | tf_op jit(solution)/shard_map/reshape | solution.py:134
  600.2 5.8 fusion.38
  606.1 3.3 collective-permute-done.10
  609.4 2.0 fusion.20
  (125 shorter events, 66.6 us)
Async XLA Ops:
  2.7 15.0 %all-to-all-start = ((s32[64,1,2]{2,1,0:T(1,128)}), s32[64,1,2]{2,1,0:T(1,128)S(1)}, u32[]{:S(2)}, u32[]{:S(2)}) async-start(s32[64,1,2]{2,1,0:T(1,128)} %bitcast.18), calls=%async_computation | async-start | bytes 65536 | tf_op jit(solution)/shard_map/all_to_all | solution.py:51
  26.5 10.5 %copy-start.3 = (bf16[256,512]{1,0:T(8,128)(2,1)S(1)}, bf16[256,512]{1,0:T(8,128)(2,1)}, u32[]{:S(2)}) copy-start(bf16[256,512]{1,0:T(8,128)(2,1)} %param.6) | copy-start | bytes 786436
  26.5 10.5 %copy-start.4 = (bf16[256,512]{1,0:T(8,128)(2,1)S(1)}, bf16[256,512]{1,0:T(8,128)(2,1)}, u32[]{:S(2)}) copy-start(bf16[256,512]{1,0:T(8,128)(2,1)} %param.7) | copy-start | bytes 786436
  26.5 263.9 %all-to-all-start.1 = ((bf16[64,2,2,128,128]{4,3,2,1,0:T(8,128)(2,1)}), bf16[64,2,2,128,128]{4,3,2,1,0:T(8,128)(2,1)}, u32[]{:S(2)}, u32[]{:S(2)}) async-start(bf16[64,2,2,128,128]{4,3,2,1,0:T(8,128)(2,1)} %bitcast.266), calls=%async_computation.1 | async-start | bytes 16777216 | tf_op jit(solution)/shard_map/all_to_all | solution.py:64
  37.8 36.0 %collective-permute-start.5 = (bf16[2,256,512]{2,1,0:T(8,128)(2,1)}, bf16[2,256,512]{2,1,0:T(8,128)(2,1)}, u32[]{:S(2)}, u32[]{:S(2)}) collective-permute-start(bf16[2,256,512]{2,1,0:T(8,128)(2,1)} %pad_maximum_fusion.1), channel_id=1, source_target_pairs={{0,128},{4,132},{8,136},{12,140},{16,144},{20,148},{24,152},{28,15... | collective-permute-start | bytes 1572872 | tf_op jit(solution)/shard_map/ppermute | solution.py:12
  41.0 57.8 %collective-permute-start.4 = (bf16[2,256,512]{2,1,0:T(8,128)(2,1)}, bf16[2,256,512]{2,1,0:T(8,128)(2,1)}, u32[]{:S(2)}, u32[]{:S(2)}) collective-permute-start(bf16[2,256,512]{2,1,0:T(8,128)(2,1)} %pad_maximum_fusion.1), channel_id=1, source_target_pairs={{0,64},{4,68},{8,72},{12,76},{16,80},{20,84},{24,88},{28,92},{32,9... | collective-permute-start | bytes 1572872 | tf_op jit(solution)/shard_map/ppermute | solution.py:12
  41.7 190.5 %collective-permute-start.3 = (bf16[2,256,512]{2,1,0:T(8,128)(2,1)}, bf16[2,256,512]{2,1,0:T(8,128)(2,1)}, u32[]{:S(2)}, u32[]{:S(2)}) collective-permute-start(bf16[2,256,512]{2,1,0:T(8,128)(2,1)} %pad_maximum_fusion.1), channel_id=1, source_target_pairs={{0,32},{4,36},{8,40},{12,44},{16,48},{20,52},{24,56},{28,60},{32,0... | collective-permute-start | bytes 1572872 | tf_op jit(solution)/shard_map/ppermute | solution.py:12
  42.2 221.4 %collective-permute-start.2 = (bf16[2,256,512]{2,1,0:T(8,128)(2,1)}, bf16[2,256,512]{2,1,0:T(8,128)(2,1)}, u32[]{:S(2)}, u32[]{:S(2)}) collective-permute-start(bf16[2,256,512]{2,1,0:T(8,128)(2,1)} %pad_maximum_fusion.1), channel_id=1, source_target_pairs={{0,16},{4,20},{8,24},{12,28},{16,0},{20,4},{24,8},{28,12},{32,48},... | collective-permute-start | bytes 1572872 | tf_op jit(solution)/shard_map/ppermute | solution.py:12
  44.6 224.4 %collective-permute-start.1 = (bf16[2,256,512]{2,1,0:T(8,128)(2,1)}, bf16[2,256,512]{2,1,0:T(8,128)(2,1)}, u32[]{:S(2)}, u32[]{:S(2)}) collective-permute-start(bf16[2,256,512]{2,1,0:T(8,128)(2,1)} %pad_maximum_fusion.1), channel_id=1, source_target_pairs={{0,8},{4,12},{8,0},{12,4},{16,24},{20,28},{24,16},{28,20},{32,40},... | collective-permute-start | bytes 1572872 | tf_op jit(solution)/shard_map/ppermute | solution.py:12
  73.8 200.4 %collective-permute-start = (bf16[2,256,512]{2,1,0:T(8,128)(2,1)}, bf16[2,256,512]{2,1,0:T(8,128)(2,1)}, u32[]{:S(2)}, u32[]{:S(2)}) collective-permute-start(bf16[2,256,512]{2,1,0:T(8,128)(2,1)} %pad_maximum_fusion.1), channel_id=1, source_target_pairs={{0,4},{4,0},{8,12},{12,8},{16,20},{20,16},{24,28},{28,24},{32,36},... | collective-permute-start | bytes 1572872 | tf_op jit(solution)/shard_map/ppermute | solution.py:12
  279.5 7.0 %copy-start.8 = (bf16[2,128,4,128]{3,2,1,0:T(4,128)(2,1)S(1)}, bf16[2,128,4,128]{3,2,1,0:T(4,128)(2,1)}, u32[]{:S(2)}) copy-start(bf16[2,128,4,128]{3,2,1,0:T(4,128)(2,1)} %reshape_squeeze.43) | copy-start | bytes 786436
  279.5 7.8 %copy-start.7 = (bf16[2,128,4,128]{3,2,1,0:T(4,128)(2,1)S(1)}, bf16[2,128,4,128]{3,2,1,0:T(4,128)(2,1)}, u32[]{:S(2)}) copy-start(bf16[2,128,4,128]{3,2,1,0:T(4,128)(2,1)} %reshape_squeeze.44) | copy-start | bytes 786436
  279.5 8.5 %copy-start.6 = (bf16[2,128,4,128]{3,2,1,0:T(4,128)(2,1)S(1)}, bf16[2,128,4,128]{3,2,1,0:T(4,128)(2,1)}, u32[]{:S(2)}) copy-start(bf16[2,128,4,128]{3,2,1,0:T(4,128)(2,1)} %reshape_squeeze.45) | copy-start | bytes 786436
  279.5 9.3 %copy-start.5 = (bf16[2,128,4,128]{3,2,1,0:T(4,128)(2,1)S(1)}, bf16[2,128,4,128]{3,2,1,0:T(4,128)(2,1)}, u32[]{:S(2)}) copy-start(bf16[2,128,4,128]{3,2,1,0:T(4,128)(2,1)} %reshape_squeeze.46) | copy-start | bytes 786436
  279.5 10.0 %copy-start.9 = (bf16[2,128,4,128]{3,2,1,0:T(4,128)(2,1)S(1)}, bf16[2,128,4,128]{3,2,1,0:T(4,128)(2,1)}, u32[]{:S(2)}) copy-start(bf16[2,128,4,128]{3,2,1,0:T(4,128)(2,1)} %reshape_squeeze.41) | copy-start | bytes 786436
  279.5 10.0 %copy-start.10 = (bf16[2,128,4,128]{3,2,1,0:T(4,128)(2,1)S(1)}, bf16[2,128,4,128]{3,2,1,0:T(4,128)(2,1)}, u32[]{:S(2)}) copy-start(bf16[2,128,4,128]{3,2,1,0:T(4,128)(2,1)} %reshape_squeeze.47) | copy-start | bytes 786436
  298.7 1.6 copy-start.1
  301.2 3.5 copy-start.11
  313.5 8.1 %copy-start = (f32[1,4,2,11,128,128]{5,4,3,2,1,0:T(8,128)}, f32[1,4,2,11,128,128]{5,4,3,2,1,0:T(8,128)S(1)}, u32[]{:S(2)}) copy-start(f32[1,4,2,11,128,128]{5,4,3,2,1,0:T(8,128)S(1)} %multiply_bitcast_fusion) | copy-start | bytes 17301508
  349.3 225.7 %all-to-all-start.2 = ((bf16[64,2,32768]{2,1,0:T(2,128)(2,1)}), bf16[64,2,32768]{2,1,0:T(2,128)(2,1)}, u32[]{:S(2)}, u32[]{:S(2)}) async-start(bf16[64,2,32768]{2,1,0:T(2,128)(2,1)} %reshape.378), calls=%async_computation.2 | async-start | bytes 16777216 | tf_op jit(solution)/shard_map/all_to_all | solution.py:128
  363.6 236.6 %collective-permute-start.9 = (bf16[2,4,2,128,128]{4,3,2,1,0:T(8,128)(2,1)}, bf16[2,4,2,128,128]{4,3,2,1,0:T(8,128)(2,1)}, u32[]{:S(2)}, u32[]{:S(2)}) collective-permute-start(bf16[2,4,2,128,128]{4,3,2,1,0:T(8,128)(2,1)} %get-tuple-element.8), channel_id=1, source_target_pairs={{0,32},{4,36},{8,40},{12,44},{16,48},{20,52},{24,56},{28,60},{32,0... | collective-permute-start | bytes 1572872 | tf_op jit(solution)/shard_map/ppermute | solution.py:12
  364.3 3.8 copy-start.12
  369.0 237.0 %collective-permute-start.8 = (bf16[2,4,2,128,128]{4,3,2,1,0:T(8,128)(2,1)}, bf16[2,4,2,128,128]{4,3,2,1,0:T(8,128)(2,1)S(1)}, u32[]{:S(2)}, u32[]{:S(2)}) collective-permute-start(bf16[2,4,2,128,128]{4,3,2,1,0:T(8,128)(2,1)} %get-tuple-element.9), channel_id=1, source_target_pairs={{0,16},{4,20},{8,24},{12,28},{16,0},{20,4},{24,8},{28,12},{32,48},... | collective-permute-start | bytes 1572872 | tf_op jit(solution)/shard_map/ppermute | solution.py:12
  371.4 234.6 %collective-permute-start.7 = (bf16[2,4,2,128,128]{4,3,2,1,0:T(8,128)(2,1)}, bf16[2,4,2,128,128]{4,3,2,1,0:T(8,128)(2,1)S(1)}, u32[]{:S(2)}, u32[]{:S(2)}) collective-permute-start(bf16[2,4,2,128,128]{4,3,2,1,0:T(8,128)(2,1)} %get-tuple-element.10), channel_id=1, source_target_pairs={{0,8},{4,12},{8,0},{12,4},{16,24},{20,28},{24,16},{28,20},{32,40},... | collective-permute-start | bytes 1572872 | tf_op jit(solution)/shard_map/ppermute | solution.py:12
  372.9 233.1 %collective-permute-start.6 = (bf16[2,4,2,128,128]{4,3,2,1,0:T(8,128)(2,1)}, bf16[2,4,2,128,128]{4,3,2,1,0:T(8,128)(2,1)S(1)}, u32[]{:S(2)}, u32[]{:S(2)}) collective-permute-start(bf16[2,4,2,128,128]{4,3,2,1,0:T(8,128)(2,1)} %get-tuple-element.11), channel_id=1, source_target_pairs={{0,4},{4,0},{8,12},{12,8},{16,20},{20,16},{24,28},{28,24},{32,36},... | collective-permute-start | bytes 1572872 | tf_op jit(solution)/shard_map/ppermute | solution.py:12
  372.9 233.1 %collective-permute-start.11 = (bf16[2,4,2,128,128]{4,3,2,1,0:T(8,128)(2,1)}, bf16[2,4,2,128,128]{4,3,2,1,0:T(8,128)(2,1)S(1)}, u32[]{:S(2)}, u32[]{:S(2)}) collective-permute-start(bf16[2,4,2,128,128]{4,3,2,1,0:T(8,128)(2,1)} %get-tuple-element.12), channel_id=1, source_target_pairs={{0,128},{4,132},{8,136},{12,140},{16,144},{20,148},{24,152},{28,15... | collective-permute-start | bytes 1572872 | tf_op jit(solution)/shard_map/ppermute | solution.py:12
  588.2 12.0 %copy-start.13 = (bf16[2,4,2,128,128]{4,3,2,1,0:T(8,128)(2,1)S(1)}, bf16[2,4,2,128,128]{4,3,2,1,0:T(8,128)(2,1)}, u32[]{:S(2)}) copy-start(bf16[2,4,2,128,128]{4,3,2,1,0:T(8,128)(2,1)} %get-tuple-element.13) | copy-start | bytes 1572868
  600.2 9.2 %collective-permute-start.10 = (bf16[2,4,2,128,128]{4,3,2,1,0:T(8,128)(2,1)S(1)}, bf16[2,4,2,128,128]{4,3,2,1,0:T(8,128)(2,1)S(1)}, u32[]{:S(2)}, u32[]{:S(2)}) collective-permute-start(bf16[2,4,2,128,128]{4,3,2,1,0:T(8,128)(2,1)S(1)} %copy-done.13), channel_id=1, source_target_pairs={{0,64},{4,68},{8,72},{12,76},{16,80},{20,84},{24,88},{28,92},{32,9... | collective-permute-start | bytes 1572872 | tf_op jit(solution)/shard_map/ppermute | solution.py:12
  600.2 9.2 %copy-start.2 = (f32[2,4,2,128,128]{4,3,2,1,0:T(8,128)S(1)}, f32[2,4,2,128,128]{4,3,2,1,0:T(8,128)}, u32[]{:S(2)}) copy-start(f32[2,4,2,128,128]{4,3,2,1,0:T(8,128)} %get-tuple-element.7) | copy-start | bytes 3145732

commit v2 on v1

--- a/solution.py
+++ b/solution.py
@@ -72,56 +72,53 @@
         heads_here, blk_count, rand_count, 2, blk_size, head_size
     )
 
-    def key_list(which):
+    def fixed_list(which):
         own = heads_first(kv_rows[which])
         parts = [own[:, :, None], own[:, ::-1, None]]
         parts += [heads_first(far_arr[which])[:, :, None] for far_arr in far_kv]
-        parts.append(rand_kv[:, :, :, which])
         return jnp.concatenate(parts, axis=2)
 
-    key_set = key_list(0)
-    value_set = key_list(1)
+    key_fix = fixed_list(0)
+    value_fix = fixed_list(1)
+    key_rnd = rand_kv[:, :, :, 0]
+    value_rnd = rand_kv[:, :, :, 1]
     query_h = heads_first(queries)
     grad_h = heads_first(out_grad)
 
-    scores = (
-        jnp.einsum("hbtd,hbksd->hbtks", query_h, key_set, preferred_element_type=f32)
-        * score_scale
+    def mm_scores(rows, key_part):
+        return jnp.einsum("hbtd,hbksd->hbtks", rows, key_part, preferred_element_type=f32)
+
+    def mm_out(weight_part, key_part):
+        return jnp.einsum("hbtks,hbksd->hbtd", weight_part, key_part, preferred_element_type=f32)
+
+    def mm_terms(weight_part, rows):
+        return jnp.einsum("hbtks,hbtd->hbksd", weight_part, rows, preferred_element_type=f32)
+
+    scores_fix = mm_scores(query_h, key_fix) * score_scale
+    scores_rnd = mm_scores(query_h, key_rnd) * score_scale
+    grad_weights_fix = mm_scores(grad_h, value_fix)
+    grad_weights_rnd = mm_scores(grad_h, value_rnd)
+    row_max = jnp.maximum(jnp.max(scores_fix, axis=(3, 4)), jnp.max(scores_rnd, axis=(3, 4)))
+    exp_sum = jnp.sum(jnp.exp(scores_fix - row_max[..., None, None]), axis=(3, 4)) + jnp.sum(
+        jnp.exp(scores_rnd - row_max[..., None, None]), axis=(3, 4)
     )
-    row_max = jnp.max(scores, axis=(3, 4))
-    log_total = row_max + jnp.log(
-        jnp.sum(jnp.exp(scores - row_max[..., None, None]), axis=(3, 4))
+    log_total = row_max + jnp.log(exp_sum)
+    weights_fix = jnp.exp(scores_fix - log_total[..., None, None])
+    weights_rnd = jnp.exp(scores_rnd - log_total[..., None, None])
+    low_fix = weights_fix.astype(jnp.bfloat16)
+    low_rnd = weights_rnd.astype(jnp.bfloat16)
+    attn_h = (mm_out(low_fix, value_fix) + mm_out(low_rnd, value_rnd)).astype(jnp.bfloat16)
+    row_delta = jnp.sum(grad_h.astype(f32) * attn_h.astype(f32), axis=3)
+    grad_scores_fix = (weights_fix * (grad_weights_fix - row_delta[..., None, None])).astype(
+        jnp.bfloat16
     )
-    weights = jnp.exp(scores - log_total[..., None, None])
-    weights_low = weights.astype(jnp.bfloat16)
-    attn_h = jnp.einsum(
-        "hbtks,hbksd->hbtd", weights_low, value_set, preferred_element_type=f32
+    grad_scores_rnd = (weights_rnd * (grad_weights_rnd - row_delta[..., None, None])).astype(
+        jnp.bfloat16
+    )
+
+    rand_low = jnp.stack(
+        [score_scale * mm_terms(grad_scores_rnd, query_h), mm_terms(low_rnd, grad_h)]
     ).astype(jnp.bfloat16)
-    row_delta = jnp.sum(grad_h.astype(f32) * attn_h.astype(f32), axis=3)
-    grad_weights = jnp.einsum("hbtd,hbksd->hbtks", grad_h, value_set, preferred_element_type=f32)
-    grad_scores = (weights * (grad_weights - row_delta[..., None, None])).astype(jnp.bfloat16)
-    grad_query_h = (
-        score_scale
-        * jnp.einsum("hbtks,hbksd->hbtd", grad_scores, key_set, preferred_element_type=f32)
-    ).astype(jnp.bfloat16)
-    key_terms = score_scale * jnp.einsum(
-        "hbtks,hbtd->hbksd", grad_scores, query_h, preferred_element_type=f32
-    )
-    value_terms = jnp.einsum(
-        "hbtks,hbtd->hbksd", weights_low, grad_h, preferred_element_type=f32
-    )
-    terms = jnp.stack([key_terms, value_terms])
-
-    grad_kv = terms[:, :, :, 0] + low(terms[:, :, :, 1])[:, :, ::-1]
-    far_first = 2
-    rand_first = far_first + far_count
-    far_low = terms[:, :, :, far_first:rand_first].astype(jnp.bfloat16)
-    for far_level in range(far_count):
-        send = far_low[:, :, :, far_level]
-        back = swapped(send, "seq", far_level)
-        grad_kv = grad_kv + back.astype(f32)
-
-    rand_low = terms[:, :, :, rand_first:].astype(jnp.bfloat16)
     rand_req = rand_low.transpose(1, 2, 3, 0, 4, 5).reshape(total_req, 2 * blk_size * head_size)
     slot_onehot = slot_match.astype(jnp.bfloat16)
     send_terms = jnp.dot(slot_onehot, rand_req, preferred_element_type=f32).astype(jnp.bfloat16)
@@ -132,16 +129,31 @@
         concat_axis=0,
         tiled=True,
     ).reshape(slot_count, 2 * blk_size * head_size)
+
+    grad_query_h = (
+        score_scale * (mm_out(grad_scores_fix, key_fix) + mm_out(grad_scores_rnd, key_rnd))
+    ).astype(jnp.bfloat16)
+    terms = jnp.stack(
+        [score_scale * mm_terms(grad_scores_fix, query_h), mm_terms(low_fix, grad_h)]
+    )
+
+    grad_kv = terms[:, :, :, 0] + low(terms[:, :, :, 1])[:, :, ::-1]
+    far_low = terms[:, :, :, 2:].astype(jnp.bfloat16)
+    for far_level in range(far_count):
+        back = swapped(far_low[:, :, :, far_level], "seq", far_level)
+        grad_kv = grad_kv + back.astype(f32)
+    grad_rows = grad_kv.transpose(0, 2, 3, 1, 4)
+
     target_rows = jnp.arange(heads_here * blk_count, dtype=jnp.int32)
     onehot = (asked_flat[None, :] == target_rows[:, None]).astype(jnp.bfloat16)
     extra = jnp.dot(onehot, slot_terms, preferred_element_type=f32)
-    extra = extra.reshape(heads_here, blk_count, 2, blk_size, head_size).transpose(2, 0, 1, 3, 4)
-    grad_kv = (grad_kv + extra).astype(jnp.bfloat16)
+    extra = extra.reshape(heads_here, blk_count, 2, blk_size, head_size).transpose(2, 1, 3, 0, 4)
+    grad_kv = (grad_rows + extra).astype(jnp.bfloat16).reshape(2, tok_rows, heads_here * head_size)
 
     attn_out = rows_back(attn_h)
     grad_queries = rows_back(grad_query_h)
-    grad_keys = rows_back(grad_kv[0])
-    grad_values = rows_back(grad_kv[1])
+    grad_keys = grad_kv[0]
+    grad_values = grad_kv[1]
     return (attn_out, grad_queries, grad_keys, grad_values)
 
 

time: 616 us -> 608 us (0.987)
  other arithmetic: 17.5 us -> 8.15 us
  waiting for transfers between devices: 402 us -> 395 us
  starting transfers between devices: 46.7 us -> 53 us
    another operation x16 -> x22, local copies, waits for them, and re-layouts: 20.9 us -> 28.8 us  [heads_first(): arr.reshape(blk_count, blk_size, heads_here, head_size)]
    another operation x1, other arithmetic: 8.09 us -> 0.75 us
    all_to_all x1, waiting for transfers between devices: 199 us -> 192 us  [local(): lax.all_to_all(send_terms.reshape(seq_devices, slot_cap, 2 * blk_size * h...]
    dot_general x6 -> x12, matrix products: 16.1 us -> 13.4 us  [the longest x4 7.76 us: mm_scores(): jnp.einsum('hbtd,hbksd->hbtks', rows, key_part, preferred_element_type=f32)]
    unnamed x48 -> x63, local copies, waits for them, and re-layouts: 16.8 us -> 14.4 us
  transfers between devices with their start and end apart: 15 -> 15, of which waited for: 7 -> 4; matrix products, arithmetic and copies ran while one was open for 15% -> 16% of each run, Pallas kernels for 0% -> 0%
where the time goes in v2:
time: 608 us; the launch traced here: 605 us
  waiting for transfers between devices  395 us (65%)
  local copies, waits for them, and re-layouts  122 us (20%)
  starting transfers between devices  53 us (9%)
  matrix products  26.4 us (4%)
  other arithmetic  8.15 us (1%)
    ppermute x12, waiting for transfers between devices, swapped(): return lax.ppermute(value, axis, pairs)  200 us
    all_to_all x1, waiting for transfers between devices, local(): lax.all_to_all(send_terms.reshape(seq_devices, slot_cap, 2 * blk_size * h...  192 us
    another operation x22, local copies, waits for them, and re-layouts, heads_first(): arr.reshape(blk_count, blk_size, heads_here, head_size)  28.8 us
    reshape x2, local copies, waits for them, and re-layouts, local(): slot_terms = lax.all_to_all(send_terms.reshape(seq_devices, slot_cap, 2 *...  25.2 us
    ppermute x12, starting transfers between devices, swapped(): return lax.ppermute(value, axis, pairs)  17.2 us
    all_to_all x1, starting transfers between devices, local(): lax.all_to_all(send_terms.reshape(seq_devices, slot_cap, 2 * blk_size * h...  15.5 us
    unnamed x63, local copies, waits for them, and re-layouts  14.4 us
    reshape x1, local copies, waits for them, and re-layouts, local(): send_terms.reshape(seq_devices, slot_cap, 2 * blk_size * head_size)  14.2 us
  transfers between devices with their start and end apart: 15, of which 4 were waited for; matrix products, arithmetic and copies ran while one was open for 16% of the time, Pallas kernels for 0%

profile of v2, /device:TPU:152, one launch (start us, length us, event | category | flops | bytes accessed | tf_op | source)
XLA Modules:
  0.0 605.2 jit_solution(299588349740229732)
XLA Ops:
  2.7 10.2 %all-to-all-start = ((s32[64,1,2]{2,1,0:T(1,128)}), s32[64,1,2]{2,1,0:T(1,128)S(1)}, u32[]{:S(2)}, u32[]{:S(2)}) async-start(s32[64,1,2]{2,1,0:T(1,128)} %bitcast.22), calls=%async_computation | async-start | bytes 65536 | tf_op jit(solution)/shard_map/all_to_all | solution.py:51
  15.1 2.6 all-to-all-done
  19.7 7.1 %gather_fusion = bf16[128,2,128,128]{3,2,1,0:T(8,128)(2,1)} fusion(bf16[2,2,128,4,128]{4,2,3,1,0:T(8,128)(2,1)S(1)} %pad_maximum_fusion.2, s32[128]{0:T(128)S(1)} %fusion.67), kind=kCustom, calls=%fused_computation | custom fusion | bytes 16778240 | tf_op jit(solution)/shard_map/gather | solution.py:63
  26.9 10.1 %all-to-all-start.1 = ((bf16[64,2,2,128,128]{4,3,2,1,0:T(8,128)(2,1)}), bf16[64,2,2,128,128]{4,3,2,1,0:T(8,128)(2,1)}, u32[]{:S(2)}, u32[]{:S(2)}) async-start(bf16[64,2,2,128,128]{4,3,2,1,0:T(8,128)(2,1)} %bitcast.309), calls=%async_computation.1 | async-start | bytes 16777216 | tf_op jit(solution)/shard_map/all_to_all | solution.py:64
  39.1 3.2 collective-permute-start.3
  48.9 2.9 collective-permute-start.5
  53.6 187.5 %collective-permute-done.1 = bf16[2,256,512]{2,1,0:T(8,128)(2,1)} collective-permute-done((bf16[2,256,512]{2,1,0:T(8,128)(2,1)}, bf16[2,256,512]{2,1,0:T(8,128)(2,1)}, u32[]{:S(2)}, u32[]{:S(2)}) %collective-permute-start.1) | collective-permute-done | bytes 524320 | tf_op jit(solution)/shard_map/ppermute | solution.py:12
  241.1 1.9 fusion.76
  245.9 12.8 %collective-permute-done.3 = bf16[2,256,512]{2,1,0:T(8,128)(2,1)} collective-permute-done((bf16[2,256,512]{2,1,0:T(8,128)(2,1)}, bf16[2,256,512]{2,1,0:T(8,128)(2,1)}, u32[]{:S(2)}, u32[]{:S(2)}) %collective-permute-start.3) | collective-permute-done | bytes 524320 | tf_op jit(solution)/shard_map/ppermute | solution.py:12
  258.7 1.9 fusion.74
  262.3 1.8 fusion.73
  265.8 1.8 fusion.72
  271.1 1.8 copy.189
  274.6 1.8 copy.190
  278.1 1.8 copy.191
  281.7 1.8 copy.192
  285.2 1.8 copy.193
  288.7 1.8 copy.194
  297.6 2.7 bitcast_reduce_fusion
  300.3 5.3 gather_fusion.1
  315.0 3.7 reshape.385
  318.7 7.1 %convolution_convert_fusion = bf16[128,32768]{1,0:T(8,128)(2,1)} fusion(bf16[24,32768]{1,0:T(8,128)(2,1)} %reshape.385, s32[24]{0:T(128)S(1)} %multiply_add_fusion.1), kind=kOutput, calls=%fused_computation.2 | convolution fusion | flops 205523968 | bytes 9961568 | tf_op jit(solution)/shard_map/dot_general | solution.py:124
  325.8 14.2 %reshape.386 = bf16[64,2,32768]{2,1,0:T(2,128)(2,1)} reshape(bf16[128,32768]{1,0:T(8,128)(2,1)} %convolution_convert_fusion) | data formatting | bytes 16777216 | tf_op jit(solution)/shard_map/reshape | solution.py:126
  340.0 15.5 %all-to-all-start.2 = ((bf16[64,2,32768]{2,1,0:T(2,128)(2,1)}), bf16[64,2,32768]{2,1,0:T(2,128)(2,1)}, u32[]{:S(2)}, u32[]{:S(2)}) async-start(bf16[64,2,32768]{2,1,0:T(2,128)(2,1)} %reshape.386), calls=%async_computation.2 | async-start | bytes 16777216 | tf_op jit(solution)/shard_map/all_to_all | solution.py:125
  355.6 4.3 fusion.1
  366.0 2.1 fusion.29
  368.1 3.1 collective-permute-start.11
  374.5 2.4 collective-permute-start.8
  379.2 191.7 %all-to-all-done.2 = bf16[64,2,32768]{2,1,0:T(2,128)(2,1)} async-done(((bf16[64,2,32768]{2,1,0:T(2,128)(2,1)}), bf16[64,2,32768]{2,1,0:T(2,128)(2,1)}, u32[]{:S(2)}, u32[]{:S(2)}) %all-to-all-start.2) | async-done | bytes 8388640 | tf_op jit(solution)/shard_map/all_to_all | solution.py:125
  570.9 13.2 %reshape.387 = bf16[128,32768]{1,0:T(8,128)(2,1)} reshape(bf16[64,2,32768]{2,1,0:T(2,128)(2,1)} %all-to-all-done.2) | data formatting | bytes 16777216 | tf_op jit(solution)/shard_map/reshape | solution.py:131
  584.1 12.0 %copy.217 = bf16[128,32768]{0,1:T(8,128)(2,1)} copy(bf16[128,32768]{1,0:T(8,128)(2,1)} %reshape.387) | data formatting | bytes 16777216 | tf_op jit(solution)/shard_map/reshape | solution.py:131
  596.1 5.8 fusion.54
  (157 shorter events, 66.4 us)
Async XLA Ops:
  2.7 15.0 %all-to-all-start = ((s32[64,1,2]{2,1,0:T(1,128)}), s32[64,1,2]{2,1,0:T(1,128)S(1)}, u32[]{:S(2)}, u32[]{:S(2)}) async-start(s32[64,1,2]{2,1,0:T(1,128)} %bitcast.22), calls=%async_computation | async-start | bytes 65536 | tf_op jit(solution)/shard_map/all_to_all | solution.py:51
  26.9 10.1 %copy-start.11 = (bf16[256,512]{1,0:T(8,128)(2,1)S(1)}, bf16[256,512]{1,0:T(8,128)(2,1)}, u32[]{:S(2)}) copy-start(bf16[256,512]{1,0:T(8,128)(2,1)} %param.6) | copy-start | bytes 786436
  26.9 10.1 %copy-start.12 = (bf16[256,512]{1,0:T(8,128)(2,1)S(1)}, bf16[256,512]{1,0:T(8,128)(2,1)}, u32[]{:S(2)}) copy-start(bf16[256,512]{1,0:T(8,128)(2,1)} %param.7) | copy-start | bytes 786436
  26.9 273.4 %all-to-all-start.1 = ((bf16[64,2,2,128,128]{4,3,2,1,0:T(8,128)(2,1)}), bf16[64,2,2,128,128]{4,3,2,1,0:T(8,128)(2,1)}, u32[]{:S(2)}, u32[]{:S(2)}) async-start(bf16[64,2,2,128,128]{4,3,2,1,0:T(8,128)(2,1)} %bitcast.309), calls=%async_computation.1 | async-start | bytes 16777216 | tf_op jit(solution)/shard_map/all_to_all | solution.py:64
  37.8 11.1 %collective-permute-start = (bf16[2,256,512]{2,1,0:T(8,128)(2,1)}, bf16[2,256,512]{2,1,0:T(8,128)(2,1)}, u32[]{:S(2)}, u32[]{:S(2)}) collective-permute-start(bf16[2,256,512]{2,1,0:T(8,128)(2,1)} %pad_maximum_fusion.1), channel_id=1, source_target_pairs={{0,4},{4,0},{8,12},{12,8},{16,20},{20,16},{24,28},{28,24},{32,36},... | collective-permute-start | bytes 1572872 | tf_op jit(solution)/shard_map/ppermute | solution.py:12
  37.9 203.1 %collective-permute-start.1 = (bf16[2,256,512]{2,1,0:T(8,128)(2,1)}, bf16[2,256,512]{2,1,0:T(8,128)(2,1)}, u32[]{:S(2)}, u32[]{:S(2)}) collective-permute-start(bf16[2,256,512]{2,1,0:T(8,128)(2,1)} %pad_maximum_fusion.1), channel_id=1, source_target_pairs={{0,8},{4,12},{8,0},{12,4},{16,24},{20,28},{24,16},{28,20},{32,40},... | collective-permute-start | bytes 1572872 | tf_op jit(solution)/shard_map/ppermute | solution.py:12
  38.5 204.4 %collective-permute-start.2 = (bf16[2,256,512]{2,1,0:T(8,128)(2,1)}, bf16[2,256,512]{2,1,0:T(8,128)(2,1)S(1)}, u32[]{:S(2)}, u32[]{:S(2)}) collective-permute-start(bf16[2,256,512]{2,1,0:T(8,128)(2,1)} %pad_maximum_fusion.1), channel_id=1, source_target_pairs={{0,16},{4,20},{8,24},{12,28},{16,0},{20,4},{24,8},{28,12},{32,48},... | collective-permute-start | bytes 1572872 | tf_op jit(solution)/shard_map/ppermute | solution.py:12
  39.1 219.6 %collective-permute-start.3 = (bf16[2,256,512]{2,1,0:T(8,128)(2,1)}, bf16[2,256,512]{2,1,0:T(8,128)(2,1)}, u32[]{:S(2)}, u32[]{:S(2)}) collective-permute-start(bf16[2,256,512]{2,1,0:T(8,128)(2,1)} %pad_maximum_fusion.1), channel_id=1, source_target_pairs={{0,32},{4,36},{8,40},{12,44},{16,48},{20,52},{24,56},{28,60},{32,0... | collective-permute-start | bytes 1572872 | tf_op jit(solution)/shard_map/ppermute | solution.py:12
  42.3 220.0 %collective-permute-start.4 = (bf16[2,256,512]{2,1,0:T(8,128)(2,1)}, bf16[2,256,512]{2,1,0:T(8,128)(2,1)}, u32[]{:S(2)}, u32[]{:S(2)}) collective-permute-start(bf16[2,256,512]{2,1,0:T(8,128)(2,1)} %pad_maximum_fusion.1), channel_id=1, source_target_pairs={{0,64},{4,68},{8,72},{12,76},{16,80},{20,84},{24,88},{28,92},{32,9... | collective-permute-start | bytes 1572872 | tf_op jit(solution)/shard_map/ppermute | solution.py:12
  48.9 216.9 %collective-permute-start.5 = (bf16[2,256,512]{2,1,0:T(8,128)(2,1)}, bf16[2,256,512]{2,1,0:T(8,128)(2,1)}, u32[]{:S(2)}, u32[]{:S(2)}) collective-permute-start(bf16[2,256,512]{2,1,0:T(8,128)(2,1)} %pad_maximum_fusion.1), channel_id=1, source_target_pairs={{0,128},{4,132},{8,136},{12,140},{16,144},{20,148},{24,152},{28,15... | collective-permute-start | bytes 1572872 | tf_op jit(solution)/shard_map/ppermute | solution.py:12
  290.5 4.0 copy-start.13
  290.5 4.7 copy-start.14
  290.5 5.5 copy-start.15
  290.5 5.5 copy-start.16
  290.5 5.6 copy-start.17
  291.3 4.9 copy-start.18
  292.0 4.2 copy-start.19
  292.8 3.5 copy-start.20
  297.6 2.7 copy-start.6
  305.6 2.7 copy-start
  340.0 230.9 %all-to-all-start.2 = ((bf16[64,2,32768]{2,1,0:T(2,128)(2,1)}), bf16[64,2,32768]{2,1,0:T(2,128)(2,1)}, u32[]{:S(2)}, u32[]{:S(2)}) async-start(bf16[64,2,32768]{2,1,0:T(2,128)(2,1)} %reshape.386), calls=%async_computation.2 | async-start | bytes 16777216 | tf_op jit(solution)/shard_map/all_to_all | solution.py:125
  366.0 5.3 copy-start.9
  368.1 227.9 %collective-permute-start.11 = (bf16[2,4,2,128,128]{4,3,2,1,0:T(8,128)(2,1)}, bf16[2,4,2,128,128]{4,3,2,1,0:T(8,128)(2,1)}, u32[]{:S(2)}, u32[]{:S(2)}) collective-permute-start(bf16[2,4,2,128,128]{4,3,2,1,0:T(8,128)(2,1)} %get-tuple-element.12), channel_id=1, source_target_pairs={{0,128},{4,132},{8,136},{12,140},{16,144},{20,148},{24,152},{28,15... | collective-permute-start | bytes 1572872 | tf_op jit(solution)/shard_map/ppermute | solution.py:12
  373.2 228.7 %collective-permute-start.10 = (bf16[2,4,2,128,128]{4,3,2,1,0:T(8,128)(2,1)}, bf16[2,4,2,128,128]{4,3,2,1,0:T(8,128)(2,1)S(1)}, u32[]{:S(2)}, u32[]{:S(2)}) collective-permute-start(bf16[2,4,2,128,128]{4,3,2,1,0:T(8,128)(2,1)} %get-tuple-element.13), channel_id=1, source_target_pairs={{0,64},{4,68},{8,72},{12,76},{16,80},{20,84},{24,88},{28,92},{32,9... | collective-permute-start | bytes 1572872 | tf_op jit(solution)/shard_map/ppermute | solution.py:12
  374.0 228.0 %collective-permute-start.9 = (bf16[2,4,2,128,128]{4,3,2,1,0:T(8,128)(2,1)}, bf16[2,4,2,128,128]{4,3,2,1,0:T(8,128)(2,1)S(1)}, u32[]{:S(2)}, u32[]{:S(2)}) collective-permute-start(bf16[2,4,2,128,128]{4,3,2,1,0:T(8,128)(2,1)} %get-tuple-element.8), channel_id=1, source_target_pairs={{0,32},{4,36},{8,40},{12,44},{16,48},{20,52},{24,56},{28,60},{32,0... | collective-permute-start | bytes 1572872 | tf_op jit(solution)/shard_map/ppermute | solution.py:12
  374.5 227.5 %collective-permute-start.8 = (bf16[2,4,2,128,128]{4,3,2,1,0:T(8,128)(2,1)}, bf16[2,4,2,128,128]{4,3,2,1,0:T(8,128)(2,1)S(1)}, u32[]{:S(2)}, u32[]{:S(2)}) collective-permute-start(bf16[2,4,2,128,128]{4,3,2,1,0:T(8,128)(2,1)} %get-tuple-element.9), channel_id=1, source_target_pairs={{0,16},{4,20},{8,24},{12,28},{16,0},{20,4},{24,8},{28,12},{32,48},... | collective-permute-start | bytes 1572872 | tf_op jit(solution)/shard_map/ppermute | solution.py:12
  376.9 225.1 %collective-permute-start.7 = (bf16[2,4,2,128,128]{4,3,2,1,0:T(8,128)(2,1)}, bf16[2,4,2,128,128]{4,3,2,1,0:T(8,128)(2,1)S(1)}, u32[]{:S(2)}, u32[]{:S(2)}) collective-permute-start(bf16[2,4,2,128,128]{4,3,2,1,0:T(8,128)(2,1)} %get-tuple-element.10), channel_id=1, source_target_pairs={{0,8},{4,12},{8,0},{12,4},{16,24},{20,28},{24,16},{28,20},{32,40},... | collective-permute-start | bytes 1572872 | tf_op jit(solution)/shard_map/ppermute | solution.py:12
  584.1 12.0 %copy-start.23 = (bf16[2,4,2,128,128]{4,3,2,1,0:T(8,128)(2,1)S(1)}, bf16[2,4,2,128,128]{4,3,2,1,0:T(8,128)(2,1)}, u32[]{:S(2)}) copy-start(bf16[2,4,2,128,128]{4,3,2,1,0:T(8,128)(2,1)} %get-tuple-element.11) | copy-start | bytes 1572868
  596.1 5.9 collective-permute-start.6
  596.1 5.9 copy-start.3
  596.1 5.9 copy-start.5
  596.1 6.1 copy-start.10
  (7 other events, 11.2 us)

commit v3 on v2

--- a/solution.py
+++ b/solution.py
@@ -119,16 +119,18 @@
     rand_low = jnp.stack(
         [score_scale * mm_terms(grad_scores_rnd, query_h), mm_terms(low_rnd, grad_h)]
     ).astype(jnp.bfloat16)
-    rand_req = rand_low.transpose(1, 2, 3, 0, 4, 5).reshape(total_req, 2 * blk_size * head_size)
+    rand_req = rand_low.transpose(1, 2, 3, 0, 4, 5).reshape(total_req, 2, blk_size, head_size)
     slot_onehot = slot_match.astype(jnp.bfloat16)
-    send_terms = jnp.dot(slot_onehot, rand_req, preferred_element_type=f32).astype(jnp.bfloat16)
+    send_terms = jnp.einsum(
+        "pn,nksd->pksd", slot_onehot, rand_req, preferred_element_type=f32
+    ).astype(jnp.bfloat16)
     slot_terms = lax.all_to_all(
-        send_terms.reshape(seq_devices, slot_cap, 2 * blk_size * head_size),
+        send_terms.reshape(seq_devices, slot_cap, 2, blk_size, head_size),
         "seq",
         split_axis=0,
         concat_axis=0,
         tiled=True,
-    ).reshape(slot_count, 2 * blk_size * head_size)
+    ).reshape(slot_count, 2, blk_size, head_size)
 
     grad_query_h = (
         score_scale * (mm_out(grad_scores_fix, key_fix) + mm_out(grad_scores_rnd, key_rnd))
@@ -146,7 +148,7 @@
 
     target_rows = jnp.arange(heads_here * blk_count, dtype=jnp.int32)
     onehot = (asked_flat[None, :] == target_rows[:, None]).astype(jnp.bfloat16)
-    extra = jnp.dot(onehot, slot_terms, preferred_element_type=f32)
+    extra = jnp.einsum("tp,pksd->tksd", onehot, slot_terms, preferred_element_type=f32)
     extra = extra.reshape(heads_here, blk_count, 2, blk_size, head_size).transpose(2, 1, 3, 0, 4)
     grad_kv = (grad_rows + extra).astype(jnp.bfloat16).reshape(2, tok_rows, heads_here * head_size)
 

time: 608 us -> 573 us (0.942)
  local copies, waits for them, and re-layouts: 122 us -> 95.1 us
  matrix products: 26.4 us -> 17.1 us
    reshape x4 -> x1, local copies, waits for them, and re-layouts: 43 us -> 7.01 us  [local(): send_terms.reshape(seq_devices, slot_cap, 2, blk_size, head_size)]
    all_to_all x0 -> x1, local copies, waits for them, and re-layouts: none -> 9.24 us  [local(): lax.all_to_all(send_terms.reshape(seq_devices, slot_cap, 2, blk_size, hea...]
    dot_general x2, matrix products: 12.9 us -> 3.7 us  [the longest x1 2.45 us: local(): jnp.einsum('pn,nksd->pksd', slot_onehot, rand_req, preferred_element_type...]
  transfers between devices with their start and end apart: 15 -> 15, of which waited for: 4 -> 5; matrix products, arithmetic and copies ran while one was open for 16% -> 13% of each run, Pallas kernels for 0% -> 0%
where the time goes in v3:
time: 573 us; the launch traced here: 570 us
  waiting for transfers between devices  395 us (69%)
  local copies, waits for them, and re-layouts  95.1 us (17%)
  starting transfers between devices  53.4 us (9%)
  matrix products  17.1 us (3%)
  other arithmetic  8.15 us (1%)
    ppermute x12, waiting for transfers between devices, swapped(): return lax.ppermute(value, axis, pairs)  201 us
    all_to_all x1, waiting for transfers between devices, local(): lax.all_to_all(send_terms.reshape(seq_devices, slot_cap, 2, blk_size, hea...  192 us
    another operation x22, local copies, waits for them, and re-layouts, heads_first(): arr.reshape(blk_count, blk_size, heads_here, head_size)  28.8 us
    ppermute x12, starting transfers between devices, swapped(): return lax.ppermute(value, axis, pairs)  17.3 us
    unnamed x63, local copies, waits for them, and re-layouts  16 us
    all_to_all x1, starting transfers between devices, local(): lax.all_to_all(send_terms.reshape(seq_devices, slot_cap, 2, blk_size, hea...  15.5 us
  transfers between devices with their start and end apart: 15, of which 5 were waited for; matrix products, arithmetic and copies ran while one was open for 13% of the time, Pallas kernels for 0%

profile of v3, /device:TPU:152, one launch (start us, length us, event | category | flops | bytes accessed | tf_op | source)
XLA Modules:
  0.0 570.2 jit_solution(1456295449978921566)
XLA Ops:
  2.7 10.2 %all-to-all-start = ((s32[64,1,2]{2,1,0:T(1,128)}), s32[64,1,2]{2,1,0:T(1,128)S(1)}, u32[]{:S(2)}, u32[]{:S(2)}) async-start(s32[64,1,2]{2,1,0:T(1,128)} %bitcast.22), calls=%async_computation | async-start | bytes 65536 | tf_op jit(solution)/shard_map/all_to_all | solution.py:51
  15.1 2.6 all-to-all-done
  19.7 6.8 %gather_fusion = bf16[128,2,128,128]{3,2,1,0:T(8,128)(2,1)} fusion(bf16[2,2,128,4,128]{4,2,3,1,0:T(8,128)(2,1)S(1)} %pad_maximum_fusion.3, s32[128]{0:T(128)S(1)} %fusion.70), kind=kCustom, calls=%fused_computation | custom fusion | bytes 16778240 | tf_op jit(solution)/shard_map/gather | solution.py:63
  26.5 10.4 %all-to-all-start.1 = ((bf16[64,2,2,128,128]{4,3,2,1,0:T(8,128)(2,1)}), bf16[64,2,2,128,128]{4,3,2,1,0:T(8,128)(2,1)}, u32[]{:S(2)}, u32[]{:S(2)}) async-start(bf16[64,2,2,128,128]{4,3,2,1,0:T(8,128)(2,1)} %bitcast.311), calls=%async_computation.1 | async-start | bytes 16777216 | tf_op jit(solution)/shard_map/all_to_all | solution.py:64
  39.1 3.2 collective-permute-start.3
  48.9 2.9 collective-permute-start.5
  51.8 1.8 fusion.80
  53.6 187.5 %collective-permute-done.1 = bf16[2,256,512]{2,1,0:T(8,128)(2,1)} collective-permute-done((bf16[2,256,512]{2,1,0:T(8,128)(2,1)}, bf16[2,256,512]{2,1,0:T(8,128)(2,1)}, u32[]{:S(2)}, u32[]{:S(2)}) %collective-permute-start.1) | collective-permute-done | bytes 524320 | tf_op jit(solution)/shard_map/ppermute | solution.py:12
  241.0 1.9 fusion.79
  245.8 12.8 %collective-permute-done.3 = bf16[2,256,512]{2,1,0:T(8,128)(2,1)} collective-permute-done((bf16[2,256,512]{2,1,0:T(8,128)(2,1)}, bf16[2,256,512]{2,1,0:T(8,128)(2,1)}, u32[]{:S(2)}, u32[]{:S(2)}) %collective-permute-start.3) | collective-permute-done | bytes 524320 | tf_op jit(solution)/shard_map/ppermute | solution.py:12
  258.6 1.9 fusion.77
  262.2 1.8 fusion.76
  265.8 1.8 fusion.75
  271.1 1.8 copy.188
  274.6 1.8 copy.189
  278.1 1.8 copy.190
  281.6 1.8 copy.191
  285.2 1.8 copy.192
  288.7 1.8 copy.193
  292.7 1.7 bitcast_dynamic-update-slice_fusion.9
  297.6 2.7 bitcast_reduce_fusion
  300.2 5.3 gather_fusion.1
  313.7 2.5 convolution_convert_fusion
  316.2 7.0 %copy.216 = bf16[64,2,2,128,128]{4,1,3,2,0:T(2,128)(2,1)} copy(bf16[64,2,2,128,128]{4,1,0,3,2:T(2,128)(2,1)S(1)} %bitcast.313) | data formatting | bytes 16777216 | tf_op jit(solution)/shard_map/reshape | solution.py:128
  323.2 15.5 %all-to-all-start.2 = ((bf16[64,2,2,128,128]{4,1,3,2,0:T(2,128)(2,1)}), bf16[64,2,2,128,128]{4,1,3,2,0:T(2,128)(2,1)}, u32[]{:S(2)}, u32[]{:S(2)}) async-start(bf16[64,2,2,128,128]{4,1,3,2,0:T(2,128)(2,1)} %copy.216), calls=%async_computation.2 | async-start | bytes 16777216 | tf_op jit(solution)/shard_map/all_to_all | solution.py:127
  338.8 4.3 fusion.1
  349.2 2.1 fusion.30
  351.4 3.1 collective-permute-start.11
  357.7 2.4 collective-permute-start.8
  362.4 191.7 %all-to-all-done.2 = bf16[64,2,2,128,128]{4,1,3,2,0:T(2,128)(2,1)} async-done(((bf16[64,2,2,128,128]{4,1,3,2,0:T(2,128)(2,1)}), bf16[64,2,2,128,128]{4,1,3,2,0:T(2,128)(2,1)}, u32[]{:S(2)}, u32[]{:S(2)}) %all-to-all-start.2) | async-done | bytes 8388640 | tf_op jit(solution)/shard_map/all_to_all | solution.py:127
  554.1 9.2 %copy.217 = bf16[64,2,2,128,128]{4,1,0,3,2:T(2,128)(2,1)S(1)} copy(bf16[64,2,2,128,128]{4,1,3,2,0:T(2,128)(2,1)} %all-to-all-done.2) | data formatting | bytes 16777216 | tf_op jit(solution)/shard_map/all_to_all | solution.py:127
  567.1 1.7 fusion.29
  (154 shorter events, 63.4 us)
Async XLA Ops:
  2.7 15.0 %all-to-all-start = ((s32[64,1,2]{2,1,0:T(1,128)}), s32[64,1,2]{2,1,0:T(1,128)S(1)}, u32[]{:S(2)}, u32[]{:S(2)}) async-start(s32[64,1,2]{2,1,0:T(1,128)} %bitcast.22), calls=%async_computation | async-start | bytes 65536 | tf_op jit(solution)/shard_map/all_to_all | solution.py:51
  26.5 10.4 %copy-start.11 = (bf16[256,512]{1,0:T(8,128)(2,1)S(1)}, bf16[256,512]{1,0:T(8,128)(2,1)}, u32[]{:S(2)}) copy-start(bf16[256,512]{1,0:T(8,128)(2,1)} %param.6) | copy-start | bytes 786436
  26.5 10.4 %copy-start.12 = (bf16[256,512]{1,0:T(8,128)(2,1)S(1)}, bf16[256,512]{1,0:T(8,128)(2,1)}, u32[]{:S(2)}) copy-start(bf16[256,512]{1,0:T(8,128)(2,1)} %param.7) | copy-start | bytes 786436
  26.5 273.7 %all-to-all-start.1 = ((bf16[64,2,2,128,128]{4,3,2,1,0:T(8,128)(2,1)}), bf16[64,2,2,128,128]{4,3,2,1,0:T(8,128)(2,1)}, u32[]{:S(2)}, u32[]{:S(2)}) async-start(bf16[64,2,2,128,128]{4,3,2,1,0:T(8,128)(2,1)} %bitcast.311), calls=%async_computation.1 | async-start | bytes 16777216 | tf_op jit(solution)/shard_map/all_to_all | solution.py:64
  37.8 11.1 %collective-permute-start = (bf16[2,256,512]{2,1,0:T(8,128)(2,1)}, bf16[2,256,512]{2,1,0:T(8,128)(2,1)}, u32[]{:S(2)}, u32[]{:S(2)}) collective-permute-start(bf16[2,256,512]{2,1,0:T(8,128)(2,1)} %pad_maximum_fusion.2), channel_id=1, source_target_pairs={{0,4},{4,0},{8,12},{12,8},{16,20},{20,16},{24,28},{28,24},{32,36},... | collective-permute-start | bytes 1572872 | tf_op jit(solution)/shard_map/ppermute | solution.py:12
  37.9 203.1 %collective-permute-start.1 = (bf16[2,256,512]{2,1,0:T(8,128)(2,1)}, bf16[2,256,512]{2,1,0:T(8,128)(2,1)}, u32[]{:S(2)}, u32[]{:S(2)}) collective-permute-start(bf16[2,256,512]{2,1,0:T(8,128)(2,1)} %pad_maximum_fusion.2), channel_id=1, source_target_pairs={{0,8},{4,12},{8,0},{12,4},{16,24},{20,28},{24,16},{28,20},{32,40},... | collective-permute-start | bytes 1572872 | tf_op jit(solution)/shard_map/ppermute | solution.py:12
  38.5 204.4 %collective-permute-start.2 = (bf16[2,256,512]{2,1,0:T(8,128)(2,1)}, bf16[2,256,512]{2,1,0:T(8,128)(2,1)S(1)}, u32[]{:S(2)}, u32[]{:S(2)}) collective-permute-start(bf16[2,256,512]{2,1,0:T(8,128)(2,1)} %pad_maximum_fusion.2), channel_id=1, source_target_pairs={{0,16},{4,20},{8,24},{12,28},{16,0},{20,4},{24,8},{28,12},{32,48},... | collective-permute-start | bytes 1572872 | tf_op jit(solution)/shard_map/ppermute | solution.py:12
  39.1 219.6 %collective-permute-start.3 = (bf16[2,256,512]{2,1,0:T(8,128)(2,1)}, bf16[2,256,512]{2,1,0:T(8,128)(2,1)}, u32[]{:S(2)}, u32[]{:S(2)}) collective-permute-start(bf16[2,256,512]{2,1,0:T(8,128)(2,1)} %pad_maximum_fusion.2), channel_id=1, source_target_pairs={{0,32},{4,36},{8,40},{12,44},{16,48},{20,52},{24,56},{28,60},{32,0... | collective-permute-start | bytes 1572872 | tf_op jit(solution)/shard_map/ppermute | solution.py:12
  42.3 220.0 %collective-permute-start.4 = (bf16[2,256,512]{2,1,0:T(8,128)(2,1)}, bf16[2,256,512]{2,1,0:T(8,128)(2,1)}, u32[]{:S(2)}, u32[]{:S(2)}) collective-permute-start(bf16[2,256,512]{2,1,0:T(8,128)(2,1)} %pad_maximum_fusion.2), channel_id=1, source_target_pairs={{0,64},{4,68},{8,72},{12,76},{16,80},{20,84},{24,88},{28,92},{32,9... | collective-permute-start | bytes 1572872 | tf_op jit(solution)/shard_map/ppermute | solution.py:12
  48.9 216.9 %collective-permute-start.5 = (bf16[2,256,512]{2,1,0:T(8,128)(2,1)}, bf16[2,256,512]{2,1,0:T(8,128)(2,1)}, u32[]{:S(2)}, u32[]{:S(2)}) collective-permute-start(bf16[2,256,512]{2,1,0:T(8,128)(2,1)} %pad_maximum_fusion.2), channel_id=1, source_target_pairs={{0,128},{4,132},{8,136},{12,140},{16,144},{20,148},{24,152},{28,15... | collective-permute-start | bytes 1572872 | tf_op jit(solution)/shard_map/ppermute | solution.py:12
  290.5 4.0 copy-start.13
  290.5 4.7 copy-start.14
  290.5 5.5 copy-start.15
  290.5 5.5 copy-start.16
  290.5 5.6 copy-start.17
  291.2 4.9 copy-start.18
  292.0 4.2 copy-start.19
  292.7 3.5 copy-start.20
  297.6 2.7 copy-start.6
  305.5 2.7 copy-start
  323.2 230.9 %all-to-all-start.2 = ((bf16[64,2,2,128,128]{4,1,3,2,0:T(2,128)(2,1)}), bf16[64,2,2,128,128]{4,1,3,2,0:T(2,128)(2,1)}, u32[]{:S(2)}, u32[]{:S(2)}) async-start(bf16[64,2,2,128,128]{4,1,3,2,0:T(2,128)(2,1)} %copy.216), calls=%async_computation.2 | async-start | bytes 16777216 | tf_op jit(solution)/shard_map/all_to_all | solution.py:127
  349.2 5.3 copy-start.9
  351.4 212.0 %collective-permute-start.11 = (bf16[2,4,2,128,128]{4,3,2,1,0:T(8,128)(2,1)}, bf16[2,4,2,128,128]{4,3,2,1,0:T(8,128)(2,1)}, u32[]{:S(2)}, u32[]{:S(2)}) collective-permute-start(bf16[2,4,2,128,128]{4,3,2,1,0:T(8,128)(2,1)} %get-tuple-element.12), channel_id=1, source_target_pairs={{0,128},{4,132},{8,136},{12,140},{16,144},{20,148},{24,152},{28,15... | collective-permute-start | bytes 1572872 | tf_op jit(solution)/shard_map/ppermute | solution.py:12
  356.4 208.3 %collective-permute-start.10 = (bf16[2,4,2,128,128]{4,3,2,1,0:T(8,128)(2,1)}, bf16[2,4,2,128,128]{4,3,2,1,0:T(8,128)(2,1)S(1)}, u32[]{:S(2)}, u32[]{:S(2)}) collective-permute-start(bf16[2,4,2,128,128]{4,3,2,1,0:T(8,128)(2,1)} %get-tuple-element.13), channel_id=1, source_target_pairs={{0,64},{4,68},{8,72},{12,76},{16,80},{20,84},{24,88},{28,92},{32,9... | collective-permute-start | bytes 1572872 | tf_op jit(solution)/shard_map/ppermute | solution.py:12
  357.2 207.6 %collective-permute-start.9 = (bf16[2,4,2,128,128]{4,3,2,1,0:T(8,128)(2,1)}, bf16[2,4,2,128,128]{4,3,2,1,0:T(8,128)(2,1)S(1)}, u32[]{:S(2)}, u32[]{:S(2)}) collective-permute-start(bf16[2,4,2,128,128]{4,3,2,1,0:T(8,128)(2,1)} %get-tuple-element.8), channel_id=1, source_target_pairs={{0,32},{4,36},{8,40},{12,44},{16,48},{20,52},{24,56},{28,60},{32,0... | collective-permute-start | bytes 1572872 | tf_op jit(solution)/shard_map/ppermute | solution.py:12
  357.7 207.7 %collective-permute-start.8 = (bf16[2,4,2,128,128]{4,3,2,1,0:T(8,128)(2,1)}, bf16[2,4,2,128,128]{4,3,2,1,0:T(8,128)(2,1)S(1)}, u32[]{:S(2)}, u32[]{:S(2)}) collective-permute-start(bf16[2,4,2,128,128]{4,3,2,1,0:T(8,128)(2,1)} %get-tuple-element.9), channel_id=1, source_target_pairs={{0,16},{4,20},{8,24},{12,28},{16,0},{20,4},{24,8},{28,12},{32,48},... | collective-permute-start | bytes 1572872 | tf_op jit(solution)/shard_map/ppermute | solution.py:12
  360.1 205.3 %collective-permute-start.7 = (bf16[2,4,2,128,128]{4,3,2,1,0:T(8,128)(2,1)}, bf16[2,4,2,128,128]{4,3,2,1,0:T(8,128)(2,1)S(1)}, u32[]{:S(2)}, u32[]{:S(2)}) collective-permute-start(bf16[2,4,2,128,128]{4,3,2,1,0:T(8,128)(2,1)} %get-tuple-element.10), channel_id=1, source_target_pairs={{0,8},{4,12},{8,0},{12,4},{16,24},{20,28},{24,16},{28,20},{32,40},... | collective-permute-start | bytes 1572872 | tf_op jit(solution)/shard_map/ppermute | solution.py:12
  362.4 200.9 %copy-start.23 = (bf16[2,4,2,128,128]{4,3,2,1,0:T(8,128)(2,1)S(1)}, bf16[2,4,2,128,128]{4,3,2,1,0:T(8,128)(2,1)}, u32[]{:S(2)}) copy-start(bf16[2,4,2,128,128]{4,3,2,1,0:T(8,128)(2,1)} %get-tuple-element.11) | copy-start | bytes 1572868
  563.4 2.0 collective-permute-start.6
  563.5 2.2 copy-start.3
  563.5 3.5 copy-start.5
  563.5 3.7 copy-start.10
  (7 other events, 11.2 us)
